TPU v7x, 128 devices: a whole 4x4x4 slice. The times are simulated.
128 devices in a mesh: tm: 16 (over z, y_lo, core), freq: 8 (over y_hi, x).
Axes of the slice: x: 4, y: 4 (y_hi: 2, y_lo: 2; y = y_hi * 2 + y_lo), z: 4, core: 2. Of those that a mesh axis runs over, the one named last changes fastest.
Arguments:
- tokens: bfloat16 [256, 128, 1024], P('tm', 'freq'), may hold values from -16 to 16
- w_query: bfloat16 [1024, 1024], replicated, may hold values from -1 to 1
- w_key: bfloat16 [1024, 1024], replicated, may hold values from -1 to 1
- w_value: bfloat16 [1024, 1024], replicated, may hold values from -0.1875 to 0.1875
- w_out: bfloat16 [1024, 1024], replicated, may hold values from -0.75 to 0.75
- d_out: bfloat16 [256, 128, 1024], P('tm', 'freq'), may hold values from -6 to 6
Outputs:
- output: bfloat16 [256, 128, 1024], P('tm', 'freq')
- input_grad: bfloat16 [256, 128, 1024], P('tm', 'freq')
- weight_grads: float32 [1024, 4, 1024], P(('tm', 'freq'))
All inputs are finite; a program needn't handle non-finite values.
Results may differ from a plain program's by a relative error of at most 0.0093.
Values may be sent and summed in bfloat16 or wider, within the bound.
No kernel may reach another device: no remote copies, remote signals or barrier semaphores. Data moves between devices by JAX's collectives and lax.ppermute only.
A program may use at most 256 MiB of HBM per device.

v0:
```python
import math

import jax
import jax.numpy as jnp
from jax import lax
from jax.sharding import PartitionSpec as P

HEADS = 8


window_reach = 6
tile_edge = 8
span_edge = 20
norm_eps = 1e-05
far_value = -1e30


def extended(array, sides, width):
    for axis, dim in sides:
        size, length = (lax.axis_size(axis), array.shape[dim])
        up = [(i, (i + 1) % size) for i in range(size - 1)]
        down = [(j, i) for i, j in up]
        last = lax.slice_in_dim(array, length - width, length, axis=dim)
        leading = lax.slice_in_dim(array, 0, width, axis=dim)
        before = lax.ppermute(last, axis, up)
        after = lax.ppermute(leading, axis, down)
        array = jnp.concatenate([before, array, after], axis=dim)
    return array


def mix(form, left_operand, right_operand):
    return jnp.einsum(form, left_operand, right_operand, preferred_element_type=jnp.float32)


def window_mask():
    query_pos = jnp.arange(tile_edge * tile_edge)
    key_pos = jnp.arange(span_edge * span_edge)
    rise_rows = (key_pos // span_edge)[None, :] - (query_pos // tile_edge)[:, None]
    rise_cols = (key_pos % span_edge)[None, :] - (query_pos % tile_edge)[:, None]
    return (
        (rise_rows >= 0)
        & (rise_rows <= 2 * window_reach)
        & (rise_cols >= 0)
        & (rise_cols <= 2 * window_reach)
    )


def pack_tiles(field_map):
    row_total, col_total = (field_map.shape[0], field_map.shape[1])
    trailing = field_map.shape[2:]
    shaped = field_map.reshape(
        (row_total // tile_edge, tile_edge, col_total // tile_edge, tile_edge) + trailing
    )
    axes_order = (0, 2, 1, 3) + tuple(range(4, shaped.ndim))
    return shaped.transpose(axes_order).reshape(
        (row_total // tile_edge * (col_total // tile_edge), tile_edge * tile_edge) + trailing
    )


def unpack_tiles(tile_stack, row_total, col_total):
    trailing = tile_stack.shape[2:]
    shaped = tile_stack.reshape(
        (row_total // tile_edge, col_total // tile_edge, tile_edge, tile_edge) + trailing
    )
    axes_order = (0, 2, 1, 3) + tuple(range(4, shaped.ndim))
    return shaped.transpose(axes_order).reshape((row_total, col_total) + trailing)


def spread_tiles(field_map, row_total, col_total):
    trailing = field_map.shape[2:]
    tile_rows = row_total // tile_edge
    tile_cols = col_total // tile_edge
    row_index = (tile_edge * jnp.arange(tile_rows))[:, None] + jnp.arange(span_edge)[None, :]
    col_index = (tile_edge * jnp.arange(tile_cols))[:, None] + jnp.arange(span_edge)[None, :]
    picked = jnp.take(field_map, row_index, axis=0)
    picked = jnp.take(picked, col_index, axis=2)
    axes_order = (0, 2, 1, 3) + tuple(range(4, picked.ndim))
    return picked.transpose(axes_order).reshape(
        (tile_rows * tile_cols, span_edge * span_edge) + trailing
    )


def group_size(tile_count):
    best_width = 1
    for candidate in range(1, 9):
        if tile_count % candidate == 0:
            best_width = candidate
    return best_width


def over_groups(group_func, members):
    tile_count = members[0].shape[0]
    best_width = group_size(tile_count)
    grouped = tuple(
        (
            member.reshape((tile_count // best_width, best_width) + member.shape[1:])
            for member in members
        )
    )
    results = lax.map(lambda group_parts: group_func(*group_parts), grouped)
    return tuple((member.reshape((tile_count,) + member.shape[2:]) for member in results))


def attend_forward(query_map, key_map, value_map, key_ok, head_count):
    row_total, col_total, model_width = query_map.shape
    head_dim = model_width // head_count
    score_scale = 1.0 / math.sqrt(head_dim)
    inside = window_mask()
    q_tiles = pack_tiles(query_map).reshape(-1, tile_edge * tile_edge, head_count, head_dim)
    k_tiles = spread_tiles(key_map, row_total, col_total).reshape(
        -1, span_edge * span_edge, head_count, head_dim
    )
    v_tiles = spread_tiles(value_map, row_total, col_total).reshape(
        -1, span_edge * span_edge, head_count, head_dim
    )
    ok_tiles = spread_tiles(key_ok, row_total, col_total)

    def one_group(q_part, k_part, v_part, ok_part):
        allowed = inside[None, None] & (ok_part[:, None, None, :] > 0.5)
        scores = mix("nqhd,nkhd->nhqk", q_part, k_part) * score_scale
        scores = jnp.where(allowed, scores, far_value)
        row_max = jnp.max(scores, axis=-1, keepdims=True)
        log_total = row_max + jnp.log(jnp.sum(jnp.exp(scores - row_max), axis=-1, keepdims=True))
        soft_weights = jnp.where(allowed, jnp.exp(scores - log_total), 0.0)
        attended = mix("nhqk,nkhd->nqhd", soft_weights.astype(jnp.bfloat16), v_part)
        return (attended, log_total[..., 0])

    attended, log_total = over_groups(one_group, (q_tiles, k_tiles, v_tiles, ok_tiles))
    attended = unpack_tiles(
        attended.reshape(-1, tile_edge * tile_edge, model_width), row_total, col_total
    )
    log_total = unpack_tiles(log_total.transpose(0, 2, 1), row_total, col_total)
    return (attended, log_total)


def attend_query_grad(query_map, key_map, value_map, key_ok, grad_map, head_count):
    row_total, col_total, model_width = query_map.shape
    head_dim = model_width // head_count
    score_scale = 1.0 / math.sqrt(head_dim)
    inside = window_mask()
    q_tiles = pack_tiles(query_map).reshape(-1, tile_edge * tile_edge, head_count, head_dim)
    g_tiles = pack_tiles(grad_map).reshape(-1, tile_edge * tile_edge, head_count, head_dim)
    k_tiles = spread_tiles(key_map, row_total, col_total).reshape(
        -1, span_edge * span_edge, head_count, head_dim
    )
    v_tiles = spread_tiles(value_map, row_total, col_total).reshape(
        -1, span_edge * span_edge, head_count, head_dim
    )
    ok_tiles = spread_tiles(key_ok, row_total, col_total)

    def one_group(q_part, g_part, k_part, v_part, ok_part):
        allowed = inside[None, None] & (ok_part[:, None, None, :] > 0.5)
        scores = mix("nqhd,nkhd->nhqk", q_part, k_part) * score_scale
        scores = jnp.where(allowed, scores, far_value)
        row_max = jnp.max(scores, axis=-1, keepdims=True)
        log_total = row_max + jnp.log(jnp.sum(jnp.exp(scores - row_max), axis=-1, keepdims=True))
        soft_weights = jnp.where(allowed, jnp.exp(scores - log_total), 0.0)
        grad_probs = mix("nqhd,nkhd->nhqk", g_part, v_part)
        spread = jnp.sum(soft_weights * grad_probs, axis=-1, keepdims=True)
        grad_scores = (soft_weights * (grad_probs - spread) * score_scale).astype(jnp.bfloat16)
        grad_query = mix("nhqk,nkhd->nqhd", grad_scores, k_part)
        return (grad_query, log_total[..., 0], spread[..., 0])

    grad_query, log_total, spread = over_groups(
        one_group, (q_tiles, g_tiles, k_tiles, v_tiles, ok_tiles)
    )
    grad_query = unpack_tiles(
        grad_query.reshape(-1, tile_edge * tile_edge, model_width), row_total, col_total
    )
    log_total = unpack_tiles(log_total.transpose(0, 2, 1), row_total, col_total)
    spread = unpack_tiles(spread.transpose(0, 2, 1), row_total, col_total)
    return (grad_query, log_total, spread)


def attend_key_grad(key_map, value_map, query_map, grad_map, log_total, spread, head_count):
    row_total, col_total, model_width = key_map.shape
    head_dim = model_width // head_count
    score_scale = 1.0 / math.sqrt(head_dim)
    inside = window_mask()
    k_tiles = pack_tiles(key_map).reshape(-1, tile_edge * tile_edge, head_count, head_dim)
    v_tiles = pack_tiles(value_map).reshape(-1, tile_edge * tile_edge, head_count, head_dim)
    q_tiles = spread_tiles(query_map, row_total, col_total).reshape(
        -1, span_edge * span_edge, head_count, head_dim
    )
    g_tiles = spread_tiles(grad_map, row_total, col_total).reshape(
        -1, span_edge * span_edge, head_count, head_dim
    )
    l_tiles = spread_tiles(log_total, row_total, col_total).transpose(0, 2, 1)
    s_tiles = spread_tiles(spread, row_total, col_total).transpose(0, 2, 1)

    def one_group(k_part, v_part, q_part, g_part, l_part, s_part):
        scores = mix("nkhd,nqhd->nhkq", k_part, q_part) * score_scale
        soft_weights = jnp.where(inside[None, None], jnp.exp(scores - l_part[:, :, None, :]), 0.0)
        grad_probs = mix("nkhd,nqhd->nhkq", v_part, g_part)
        grad_scores = (soft_weights * (grad_probs - s_part[:, :, None, :]) * score_scale).astype(
            jnp.bfloat16
        )
        grad_keys = mix("nhkq,nqhd->nkhd", grad_scores, q_part)
        grad_values = mix("nhkq,nqhd->nkhd", soft_weights.astype(jnp.bfloat16), g_part)
        return (grad_keys, grad_values)

    grad_keys, grad_values = over_groups(
        one_group, (k_tiles, v_tiles, q_tiles, g_tiles, l_tiles, s_tiles)
    )
    grad_keys = unpack_tiles(
        grad_keys.reshape(-1, tile_edge * tile_edge, model_width), row_total, col_total
    )
    grad_values = unpack_tiles(
        grad_values.reshape(-1, tile_edge * tile_edge, model_width), row_total, col_total
    )
    return (grad_keys, grad_values)


def layer_norm(flat_rows):
    wide_values = flat_rows.astype(jnp.float32)
    center = jnp.mean(wide_values, axis=-1, keepdims=True)
    shifted = wide_values - center
    inverse = lax.rsqrt(jnp.mean(shifted * shifted, axis=-1, keepdims=True) + norm_eps)
    return (shifted * inverse, inverse)


def local(tokens, w_query, w_key, w_value, w_out, d_out):
    tile_rows, tile_cols, model_width = tokens.shape
    flat_rows = tokens.reshape(tile_rows * tile_cols, model_width)
    normed, inverse = layer_norm(flat_rows)
    hidden = normed.astype(jnp.bfloat16)
    query_rows = jnp.dot(hidden, w_query, preferred_element_type=jnp.float32).astype(jnp.bfloat16)
    key_rows = jnp.dot(hidden, w_key, preferred_element_type=jnp.float32).astype(jnp.bfloat16)
    value_rows = jnp.dot(hidden, w_value, preferred_element_type=jnp.float32).astype(jnp.bfloat16)
    query_map = query_rows.reshape(tile_rows, tile_cols, model_width)
    key_map = key_rows.reshape(tile_rows, tile_cols, model_width)
    value_map = value_rows.reshape(tile_rows, tile_cols, model_width)
    time_all = tile_rows * lax.axis_size("tm")
    freq_all = tile_cols * lax.axis_size("freq")
    time_start = lax.axis_index("tm") * tile_rows
    freq_start = lax.axis_index("freq") * tile_cols

    def inside_map(margin):
        time_pos = time_start - margin + jnp.arange(tile_rows + 2 * margin)
        freq_pos = freq_start - margin + jnp.arange(tile_cols + 2 * margin)
        time_ok = (time_pos >= 0) & (time_pos < time_all)
        freq_ok = (freq_pos >= 0) & (freq_pos < freq_all)
        return (time_ok[:, None] & freq_ok[None, :]).astype(jnp.float32)

    kv_pair = jnp.stack([key_map, value_map])
    near_rim = extended(kv_pair, (("tm", 1), ("freq", 2)), 6)
    attended, unused = attend_forward(query_map, near_rim[0], near_rim[1], inside_map(6), HEADS)
    attended_rows = attended.astype(jnp.bfloat16).reshape(tile_rows * tile_cols, model_width)
    output = (
        flat_rows.astype(jnp.float32)
        + jnp.dot(attended_rows, w_out, preferred_element_type=jnp.float32)
    ).astype(jnp.bfloat16)
    grad_flat = d_out.reshape(tile_rows * tile_cols, model_width)
    grad_att = jnp.dot(grad_flat, w_out.T, preferred_element_type=jnp.float32).astype(jnp.bfloat16)
    grad_att_map = grad_att.reshape(tile_rows, tile_cols, model_width)
    query_pair = jnp.stack([query_map, grad_att_map])
    beside_all = extended(query_pair, (("tm", 1), ("freq", 2)), 6)
    grad_query_tile, log_own, spread_own = attend_query_grad(
        query_map, near_rim[0], near_rim[1], inside_map(6), grad_att_map, HEADS
    )
    grad_query = grad_query_tile.astype(jnp.bfloat16).reshape(tile_rows * tile_cols, model_width)
    stats_pair = extended(jnp.stack([log_own, spread_own]), (("tm", 1), ("freq", 2)), 6)
    log_rim = stats_pair[0]
    spread_rim = stats_pair[1]
    grad_keys, grad_values = attend_key_grad(
        key_map, value_map, beside_all[0], beside_all[1], log_rim, spread_rim, HEADS
    )
    grad_keys = grad_keys.astype(jnp.bfloat16).reshape(tile_rows * tile_cols, model_width)
    grad_values = grad_values.astype(jnp.bfloat16).reshape(tile_rows * tile_cols, model_width)
    contract_dims = (((0,), (0,)), ((), ()))
    term_list = [
        lax.dot_general(hidden, grad_query, contract_dims, preferred_element_type=jnp.float32),
        lax.dot_general(hidden, grad_keys, contract_dims, preferred_element_type=jnp.float32),
        lax.dot_general(hidden, grad_values, contract_dims, preferred_element_type=jnp.float32),
        lax.dot_general(
            attended_rows, grad_flat, contract_dims, preferred_element_type=jnp.float32
        ),
    ]
    weight_grads = lax.psum_scatter(
        jnp.stack(term_list, axis=1), ("tm", "freq"), scatter_dimension=0, tiled=True
    )
    grad_hidden = jnp.dot(grad_query, w_query.T, preferred_element_type=jnp.float32)
    grad_hidden = grad_hidden + jnp.dot(grad_keys, w_key.T, preferred_element_type=jnp.float32)
    grad_hidden = grad_hidden + jnp.dot(grad_values, w_value.T, preferred_element_type=jnp.float32)
    center_grad = jnp.mean(grad_hidden, axis=-1, keepdims=True)
    along = jnp.mean(grad_hidden * normed, axis=-1, keepdims=True)
    input_grad = (
        grad_flat.astype(jnp.float32) + (grad_hidden - center_grad - normed * along) * inverse
    ).astype(jnp.bfloat16)
    return (
        output.reshape(tile_rows, tile_cols, model_width),
        input_grad.reshape(tile_rows, tile_cols, model_width),
        weight_grads,
    )


def solution(mesh):
    in_specs = (P("tm", "freq", None), P(), P(), P(), P(), P("tm", "freq", None))
    out_specs = (P("tm", "freq", None), P("tm", "freq", None), P(("tm", "freq"), None, None))
    return jax.shard_map(local, mesh=mesh, in_specs=in_specs, out_specs=out_specs, check_vma=False)
```

profile of v0, /device:TPU:0, one launch (start us, length us, event | category | flops | bytes accessed | tf_op | source)
XLA Modules:
  0.0 1072.4 jit_solution(9218039446161331931)
XLA Ops:
  22.1 5.7 collective-permute-start
  49.1 4.6 collective-permute-start.2
  63.3 5.6 collective-permute-start.6
  75.1 3.8 gather_fusion.4
  90.9 3.9 gather_fusion.10
  94.8 3.9 gather_fusion.6
  98.7 3.9 gather_fusion
  102.7 17.8 %broadcast_select_fusion.4 = (bf16[2,20,28,1024]{3,0,2,1:T(2,128)(2,1)}, bf16[2,20,28,1024]{3,0,2,1:T(2,128)(2,1)}, bf16[2,20,28,1024]{3,0,2,1:T(2,128)(2,1)}, bf16[2,20,28,1024]{3,0,2,1:T(2,128)(2,1)}) fusion(pred[2,20]{0,1:T(8,128)(4,1)S(1)} %copy-done.48, bf16[2,20,28,1024]{3,2,1,0:T(8,128)(2,1)} %bitcast.194, bf16[2,20,28,1024]{3,2,1,0:T(8,128)(2,1)} %bitcast.193, ...), kind=kLoop, calls=%fused_computation.19 | loop fusion | flops 4587520 | bytes 18350120 | tf_op jit(solution)/shard_map/jit(_take)/select_n | solution.py:75
  120.5 11.7 %gather_fusion.11 = bf16[40,2,20,1024]{3,1,2,0:T(2,128)(2,1)} fusion(bf16[2,20,28,1024]{3,0,2,1:T(2,128)(2,1)} %get-tuple-element.125, s32[1024]{0:T(1024)S(1)} %copy-done.36), kind=kCustom, calls=%fused_computation.11.clone | custom fusion | bytes 6553760 | tf_op jit(solution)/shard_map/jit(_take)/gather | solution.py:76
  132.2 12.1 %gather_fusion.5 = bf16[40,2,20,1024]{3,1,2,0:T(2,128)(2,1)} fusion(bf16[2,20,28,1024]{3,0,2,1:T(2,128)(2,1)} %get-tuple-element.126, s32[1024]{0:T(1024)S(1)} %copy-done.36), kind=kCustom, calls=%fused_computation.9.clone | custom fusion | bytes 6553760 | tf_op jit(solution)/shard_map/jit(_take)/gather | solution.py:76
  144.4 11.7 %gather_fusion.7 = bf16[40,2,20,1024]{3,1,2,0:T(2,128)(2,1)} fusion(bf16[2,20,28,1024]{3,0,2,1:T(2,128)(2,1)} %get-tuple-element.127, s32[1024]{0:T(1024)S(1)} %copy-done.36), kind=kCustom, calls=%fused_computation.10.clone | custom fusion | bytes 6553760 | tf_op jit(solution)/shard_map/jit(_take)/gather | solution.py:76
  156.1 11.7 %gather_fusion.1 = bf16[40,2,20,1024]{3,1,2,0:T(2,128)(2,1)} fusion(bf16[2,20,28,1024]{3,0,2,1:T(2,128)(2,1)} %get-tuple-element.128, s32[1024]{0:T(1024)S(1)} %copy-done.36), kind=kCustom, calls=%fused_computation.1.clone | custom fusion | bytes 6553760 | tf_op jit(solution)/shard_map/jit(_take)/gather | solution.py:76
  167.8 15.7 %fusion.3 = (bf16[2,2,20,20,1024]{4,0,2,3,1:T(2,128)(2,1)}, bf16[2,2,20,20,1024]{4,0,2,3,1:T(2,128)(2,1)S(1)}, bf16[2,2,20,20,1024]{4,0,2,3,1:T(2,128)(2,1)}, bf16[2,2,20,20,1024]{4,0,2,3,1:T(2,128)(2,1)}) fusion(bf16[2,20,2,20,1024]{4,2,3,1,0:T(2,128)(2,1)} %bitcast.189, pred[2,20]{1,0:T(4,128)(4,1)S(1)} %copy-done.42, ...), kind=kLoop, calls=%fused_computation.35 | loop fusion | flops 6553600 | bytes 26214440 | tf_op jit(solution)/shard_map/transpose | solution.py:78
  183.5 6.8 copy.164
  190.4 8.2 squeeze.76
  198.6 8.7 copy.183
  207.3 8.4 squeeze.79
  215.7 8.7 copy.156
  224.4 8.6 squeeze.73
  233.0 5.6 fusion.4
  242.2 6.8 fusion.68
  254.1 8.0 multiply_reduce_fusion
  262.1 5.2 fusion.73
  271.5 4.1 convolution_bitcast_fusion
  275.6 4.6 fusion.6
  285.4 4.2 collective-permute-start.10
  293.7 6.8 copy.196
  300.5 8.4 squeeze.84
  326.8 6.6 fusion.63
  338.6 11.3 %fusion.58 = bf16[4,64,8,128]{3,1,2,0:T(8,128)(2,1)} fusion(bf16[4,400,8,128]{3,2,0,1:T(8,128)(2,1)} %squeeze.79, f32[4,8,64,400]{3,2,1,0:T(8,128)} %fusion.6, f32[4,8,400]{2,1,0:T(8,128)S(1)} %bitcast.244, f32[4,8,400]{2,1,0:T(8,128)S(1)} %bitcast.243, pred[64,400]{1,0:T(8,128)(4,1)S(1)} %copy-done.35, bf16[4,400,8,128]{3,2,0,1:T(8,128)(2,1)} %squeeze.84, ...), kind=kOutput, calls=%fused_computation.88 | convolution fusion | flops 425426944 | bytes 11006976 | tf_op jit(solution)/shard_map/while/body/eval_jaxpr/nhkq,nqhd->nkhd/dot_general | solution.py:32
  359.5 6.1 pad_maximum_fusion
  375.7 687.8 %reduce-scatter.2.cloned.1.call-done = f32[8,4,1024]{2,0,1:T(8,128)} async-done(((f32[1024,4,1024]{2,0,1:T(8,128)}), f32[8,4,1024]{2,0,1:T(8,128)}) %reduce-scatter.2.cloned.1.call-update) | async-done | bytes 131088 | tf_op jit(solution)/shard_map/reduce_scatter | solution.py:279
  (233 shorter events, 129.7 us)
Async XLA Ops:
  7.2 12.3 %copy-start = (bf16[1024,1024]{1,0:T(8,128)(2,1)S(1)}, bf16[1024,1024]{1,0:T(8,128)(2,1)}, u32[]{:S(2)}) copy-start(bf16[1024,1024]{1,0:T(8,128)(2,1)} %param.21) | copy-start | bytes 6291460
  7.2 1056.3 %reduce-scatter.2.cloned.1.call-start = ((), (), s32[]{:S(2)}) async-start(), calls=%async_computation.1 | async-start | bytes 16908288 | tf_op jit(solution)/shard_map/reduce_scatter | solution.py:279
  15.7 26.0 %copy-start.8 = (bf16[256,1024]{1,0:T(8,128)(2,1)}, bf16[256,1024]{1,0:T(8,128)(2,1)S(1)}, u32[]{:S(2)}) copy-start(bf16[256,1024]{1,0:T(8,128)(2,1)S(1)} %convolution_convert_fusion) | copy-start | bytes 1572868
  16.7 40.5 %collective-permute-start.4 = (bf16[2,6,16,1024]{3,2,1,0:T(8,128)(2,1)}, bf16[2,6,16,1024]{3,2,1,0:T(8,128)(2,1)S(1)}, u32[]{:S(2)}, u32[]{:S(2)}) collective-permute-start(bf16[2,6,16,1024]{3,2,1,0:T(8,128)(2,1)} %get-tuple-element.115), channel_id=1, source_target_pairs={{0,8},{8,16},{16,24},{24,32},{32,40},{40,48},{48,56},{56,64},{64,7... | collective-permute-start | bytes 1179656 | tf_op jit(solution)/shard_map/ppermute | solution.py:25
  18.2 39.1 %collective-permute-start.5 = (bf16[2,6,16,1024]{3,2,1,0:T(8,128)(2,1)}, bf16[2,6,16,1024]{3,2,1,0:T(8,128)(2,1)}, u32[]{:S(2)}, u32[]{:S(2)}) collective-permute-start(bf16[2,6,16,1024]{3,2,1,0:T(8,128)(2,1)} %get-tuple-element.116), channel_id=1, source_target_pairs={{8,0},{16,8},{24,16},{32,24},{40,32},{48,40},{56,48},{64,56},{72,6... | collective-permute-start | bytes 1179656 | tf_op jit(solution)/shard_map/ppermute | solution.py:26
  20.2 23.2 %copy-start.1 = (bf16[16,16,1024]{2,1,0:T(8,128)(2,1)S(1)}, bf16[16,16,1024]{2,1,0:T(8,128)(2,1)}, u32[]{:S(2)}) copy-start(bf16[16,16,1024]{2,1,0:T(8,128)(2,1)} %param.18) | copy-start | bytes 1572868
  22.1 22.4 %collective-permute-start = (bf16[2,6,16,1024]{3,2,1,0:T(8,128)(2,1)}, bf16[2,6,16,1024]{3,2,1,0:T(8,128)(2,1)}, u32[]{:S(2)}, u32[]{:S(2)}) collective-permute-start(bf16[2,6,16,1024]{3,2,1,0:T(8,128)(2,1)} %get-tuple-element.117), channel_id=1, source_target_pairs={{0,8},{8,16},{16,24},{24,32},{32,40},{40,48},{48,56},{56,64},{64,7... | collective-permute-start | bytes 1179656 | tf_op jit(solution)/shard_map/ppermute | solution.py:25
  27.7 16.8 %collective-permute-start.1 = (bf16[2,6,16,1024]{3,2,1,0:T(8,128)(2,1)}, bf16[2,6,16,1024]{3,2,1,0:T(8,128)(2,1)}, u32[]{:S(2)}, u32[]{:S(2)}) collective-permute-start(bf16[2,6,16,1024]{3,2,1,0:T(8,128)(2,1)} %get-tuple-element.118), channel_id=1, source_target_pairs={{8,0},{16,8},{24,16},{32,24},{40,32},{48,40},{56,48},{64,56},{72,6... | collective-permute-start | bytes 1179656 | tf_op jit(solution)/shard_map/ppermute | solution.py:26
  43.5 13.0 %copy-start.34 = (pred[64,400]{1,0:T(8,128)(4,1)}, pred[64,400]{1,0:T(8,128)(4,1)S(1)}, u32[]{:S(2)}) copy-start(pred[64,400]{1,0:T(8,128)(4,1)S(1)} %fusion.85) | copy-start | bytes 76804
  46.9 8.7 copy-start.6
  47.7 9.6 copy-start.9
  47.7 21.2 %collective-permute-start.3 = (bf16[2,28,6,1024]{3,0,2,1:T(2,128)(2,1)S(1)}, bf16[2,28,6,1024]{3,0,2,1:T(2,128)(2,1)S(1)}, u32[]{:S(2)}, u32[]{:S(2)}) collective-permute-start(bf16[2,28,6,1024]{3,0,2,1:T(2,128)(2,1)S(1)} %copy.151), channel_id=1, source_target_pairs={{1,0},{2,1},{3,2},{4,3},{5,4},{6,5},{7,6},{9,8},{10,9},{11,10},{12... | collective-permute-start | bytes 2064392 | tf_op jit(solution)/shard_map/ppermute | solution.py:26
  49.1 20.0 %collective-permute-start.2 = (bf16[2,28,6,1024]{3,0,2,1:T(2,128)(2,1)S(1)}, bf16[2,28,6,1024]{3,0,2,1:T(2,128)(2,1)S(1)}, u32[]{:S(2)}, u32[]{:S(2)}) collective-permute-start(bf16[2,28,6,1024]{3,0,2,1:T(2,128)(2,1)S(1)} %copy.150), channel_id=1, source_target_pairs={{0,1},{1,2},{2,3},{3,4},{4,5},{5,6},{6,7},{8,9},{9,10},{10,11},{11... | collective-permute-start | bytes 2064392 | tf_op jit(solution)/shard_map/ppermute | solution.py:25
  62.0 20.5 %collective-permute-start.7 = (bf16[2,28,6,1024]{3,0,2,1:T(2,128)(2,1)}, bf16[2,28,6,1024]{3,0,2,1:T(2,128)(2,1)}, u32[]{:S(2)}, u32[]{:S(2)}) collective-permute-start(bf16[2,28,6,1024]{3,0,2,1:T(2,128)(2,1)} %copy.178), channel_id=1, source_target_pairs={{1,0},{2,1},{3,2},{4,3},{5,4},{6,5},{7,6},{9,8},{10,9},{11,10},{12... | collective-permute-start | bytes 2064392 | tf_op jit(solution)/shard_map/ppermute | solution.py:26
  63.3 20.7 %collective-permute-start.6 = (bf16[2,28,6,1024]{3,0,2,1:T(2,128)(2,1)}, bf16[2,28,6,1024]{3,0,2,1:T(2,128)(2,1)}, u32[]{:S(2)}, u32[]{:S(2)}) collective-permute-start(bf16[2,28,6,1024]{3,0,2,1:T(2,128)(2,1)} %copy.177), channel_id=1, source_target_pairs={{0,1},{1,2},{2,3},{3,4},{4,5},{5,6},{6,7},{8,9},{9,10},{10,11},{11... | collective-permute-start | bytes 2064392 | tf_op jit(solution)/shard_map/ppermute | solution.py:25
  79.0 6.3 copy-start.7
  79.0 6.3 copy-start.10
  156.1 11.7 %copy-start.42 = (pred[2,20]{1,0:T(4,128)(4,1)S(1)}, pred[2,20]{1,0:T(4,128)(4,1)}, u32[]{:S(2)}) copy-start(pred[2,20]{1,0:T(4,128)(4,1)} %copy-done.41) | copy-start | bytes 124
  224.4 8.6 copy-start.29
  254.1 8.0 copy-start.21
  254.1 8.0 copy-start.23
  267.7 16.8 %collective-permute-start.8 = (f32[2,6,16,8]{2,3,1,0:T(8,128)S(1)}, f32[2,6,16,8]{2,3,1,0:T(8,128)S(1)}, u32[]{:S(2)}, u32[]{:S(2)}) collective-permute-start(f32[2,6,16,8]{2,3,1,0:T(8,128)S(1)} %get-tuple-element.123), channel_id=1, source_target_pairs={{0,8},{8,16},{16,24},{24,32},{32,40},{40,48},{48,56},{56,64},{64,7... | collective-permute-start | bytes 18440 | tf_op jit(solution)/shard_map/ppermute | solution.py:25
  270.1 14.4 %collective-permute-start.9 = (f32[2,6,16,8]{2,3,1,0:T(8,128)S(1)}, f32[2,6,16,8]{2,3,1,0:T(8,128)S(1)}, u32[]{:S(2)}, u32[]{:S(2)}) collective-permute-start(f32[2,6,16,8]{2,3,1,0:T(8,128)S(1)} %get-tuple-element.124), channel_id=1, source_target_pairs={{8,0},{16,8},{24,16},{32,24},{40,32},{48,40},{56,48},{64,56},{72,6... | collective-permute-start | bytes 18440 | tf_op jit(solution)/shard_map/ppermute | solution.py:26
  284.5 9.2 copy-start.15
  284.6 9.1 copy-start.4
  285.4 23.4 %collective-permute-start.10 = (f32[2,28,6,8]{2,3,1,0:T(8,128)}, f32[2,28,6,8]{2,3,1,0:T(8,128)S(1)}, u32[]{:S(2)}, u32[]{:S(2)}) collective-permute-start(f32[2,28,6,8]{2,3,1,0:T(8,128)} %get-tuple-element.121), channel_id=1, source_target_pairs={{0,1},{1,2},{2,3},{3,4},{4,5},{5,6},{6,7},{8,9},{9,10},{10,11},{11... | collective-permute-start | bytes 32264 | tf_op jit(solution)/shard_map/ppermute | solution.py:25
  289.7 19.2 %collective-permute-start.11 = (f32[2,28,6,8]{2,3,1,0:T(8,128)}, f32[2,28,6,8]{2,3,1,0:T(8,128)}, u32[]{:S(2)}, u32[]{:S(2)}) collective-permute-start(f32[2,28,6,8]{2,3,1,0:T(8,128)} %get-tuple-element.122), channel_id=1, source_target_pairs={{1,0},{2,1},{3,2},{4,3},{5,4},{6,5},{7,6},{9,8},{10,9},{11,10},{12... | collective-permute-start | bytes 32264 | tf_op jit(solution)/shard_map/ppermute | solution.py:26
  326.8 11.8 %copy-start.35 = (pred[64,400]{1,0:T(8,128)(4,1)S(1)}, pred[64,400]{1,0:T(8,128)(4,1)}, u32[]{:S(2)}) copy-start(pred[64,400]{1,0:T(8,128)(4,1)} %copy-done.34) | copy-start | bytes 76804
  326.8 11.8 %copy-start.39 = (f32[4,400,8]{1,2,0:T(8,128)S(1)}, f32[4,400,8]{1,2,0:T(8,128)}, u32[]{:S(2)}) copy-start(f32[4,400,8]{1,2,0:T(8,128)} %reshape.304) | copy-start | bytes 153604
  326.8 11.8 %copy-start.40 = (f32[4,400,8]{1,2,0:T(8,128)S(1)}, f32[4,400,8]{1,2,0:T(8,128)}, u32[]{:S(2)}) copy-start(f32[4,400,8]{1,2,0:T(8,128)} %reshape.305) | copy-start | bytes 153604
  366.7 5.6 copy-start.19
  366.7 5.6 copy-start.25
  (31 other events, 76.3 us)
Sparse Core Ops, SparseCore 0:
  365.8 697.5 reduce-scatter.1
where the time goes:
time: 1080 us; the launch traced here: 1070 us
  waiting for transfers between devices  691 us (64%)
  local copies, waits for them, and re-layouts  195 us (18%)
  matrix products  69.6 us (6%)
  other arithmetic  68.8 us (6%)
  starting transfers between devices  31.8 us (3%)
  between operations  15.5 us (1%)
    reduce_scatter x1, waiting for transfers between devices, local(): lax.psum_scatter(jnp.stack(term_list, axis=1), ('tm', 'freq'), scatter_di...  688 us
    gather x10, local copies, waits for them, and re-layouts, spread_tiles(): picked = jnp.take(picked, col_index, axis=2)  57.8 us
    dot_general x7, matrix products, mix(): jnp.einsum(form, left_operand, right_operand, preferred_element_type=jnp....  48.1 us
    squeeze x4, local copies, waits for them, and re-layouts, over_groups(): results = lax.map(lambda group_parts: group_func(*group_parts), grouped)  33.5 us
    transpose x6, local copies, waits for them, and re-layouts, spread_tiles(): picked.transpose(axes_order)  32.3 us
    ppermute x6, starting transfers between devices, extended(): before = lax.ppermute(last, axis, up)  23.9 us
    gather x11, local copies, waits for them, and re-layouts, spread_tiles(): picked = jnp.take(field_map, row_index, axis=0)  22.9 us
  transfers between devices with their start and end apart: 13, of which 3 were waited for; matrix products, arithmetic and copies ran while one was open for 7% of the time, Pallas kernels for 0%

commit v1 on v0

--- a/solution.py
+++ b/solution.py
@@ -268,16 +268,22 @@
     grad_keys = grad_keys.astype(jnp.bfloat16).reshape(tile_rows * tile_cols, model_width)
     grad_values = grad_values.astype(jnp.bfloat16).reshape(tile_rows * tile_cols, model_width)
     contract_dims = (((0,), (0,)), ((), ()))
-    term_list = [
-        lax.dot_general(hidden, grad_query, contract_dims, preferred_element_type=jnp.float32),
-        lax.dot_general(hidden, grad_keys, contract_dims, preferred_element_type=jnp.float32),
-        lax.dot_general(hidden, grad_values, contract_dims, preferred_element_type=jnp.float32),
-        lax.dot_general(
-            attended_rows, grad_flat, contract_dims, preferred_element_type=jnp.float32
-        ),
-    ]
-    weight_grads = lax.psum_scatter(
-        jnp.stack(term_list, axis=1), ("tm", "freq"), scatter_dimension=0, tiled=True
+
+    def scatter_rows(term):
+        return lax.psum_scatter(term, ("tm", "freq"), scatter_dimension=0, tiled=True)
+
+    out_term = scatter_rows(
+        lax.dot_general(attended_rows, grad_flat, contract_dims, preferred_element_type=jnp.float32)
+    )
+    query_term = scatter_rows(
+        lax.dot_general(hidden, grad_query, contract_dims, preferred_element_type=jnp.float32)
+    )
+    kv_rows = jnp.concatenate([grad_keys, grad_values], axis=1)
+    kv_term = scatter_rows(
+        lax.dot_general(hidden, kv_rows, contract_dims, preferred_element_type=jnp.float32)
+    )
+    weight_grads = jnp.stack(
+        [query_term, kv_term[:, :model_width], kv_term[:, model_width:], out_term], axis=1
     )
     grad_hidden = jnp.dot(grad_query, w_query.T, preferred_element_type=jnp.float32)
     grad_hidden = grad_hidden + jnp.dot(grad_keys, w_key.T, preferred_element_type=jnp.float32)

time: 1080 us -> 2320 us (2.15)
  waiting for transfers between devices: 691 us -> 1920 us
    reduce_scatter x1 -> x3, waiting for transfers between devices: 688 us -> 1920 us  [scatter_rows(): lax.psum_scatter(term, ('tm', 'freq'), scatter_dimension=0, tiled=True)]
  transfers between devices with their start and end apart: 13 -> 15, of which waited for: 3 -> 4; matrix products, arithmetic and copies ran while one was open for 7% -> 6% of each run, Pallas kernels for 0% -> 0%
where the time goes in v1:
time: 2320 us; the launch traced here: 2310 us
  waiting for transfers between devices  1920 us (83%)
  local copies, waits for them, and re-layouts  194 us (8%)
  matrix products  81.5 us (4%)
  other arithmetic  62.7 us (3%)
  starting transfers between devices  36.4 us (2%)
    reduce_scatter x3, waiting for transfers between devices, scatter_rows(): lax.psum_scatter(term, ('tm', 'freq'), scatter_dimension=0, tiled=True)  1920 us
    dot_general x7, matrix products, mix(): jnp.einsum(form, left_operand, right_operand, preferred_element_type=jnp....  55.9 us
    gather x10, local copies, waits for them, and re-layouts, spread_tiles(): picked = jnp.take(picked, col_index, axis=2)  54.4 us
  transfers between devices with their start and end apart: 15, of which 4 were waited for; matrix products, arithmetic and copies ran while one was open for 6% of the time, Pallas kernels for 0%

profile of v1, /device:TPU:0, one launch (start us, length us, event | category | flops | bytes accessed | tf_op | source)
XLA Modules:
  0.0 2313.3 jit_solution(3442037576661581777)
XLA Ops:
  24.6 3.9 collective-permute-start
  49.4 5.4 collective-permute-start.6
  67.7 5.8 collective-permute-start.2
  94.7 3.9 gather_fusion.4
  98.5 3.9 gather_fusion.6
  102.4 3.9 gather_fusion
  106.4 17.8 broadcast_select_fusion.4
  124.1 11.7 gather_fusion.11
  135.9 11.9 gather_fusion.5
  147.8 11.7 gather_fusion.7
  159.5 11.7 gather_fusion.1
  171.2 15.7 fusion.3
  186.9 6.8 copy.156
  193.7 8.2 squeeze.73
  201.9 8.8 copy.164
  210.6 8.6 squeeze.76
  219.2 5.6 fusion.4
  228.5 10.1 multiply_reduce_fusion
  247.4 6.7 copy.183
  254.1 8.2 squeeze.79
  264.6 5.9 collective-permute-start.10
  270.5 6.6 fusion.6
  277.1 6.8 copy.196
  284.0 8.4 squeeze.84
  301.8 7.5 fusion.63
  309.2 10.9 fusion.58
  330.2 5.6 fusion.76
  336.8 6.8 fusion.68
  354.3 8.5 fusion.73
  380.9 627.0 %reduce-scatter.6.cloned.1.call-done = f32[8,2048]{1,0:T(8,128)} async-done(((f32[1024,2048]{1,0:T(8,128)}), f32[8,2048]{1,0:T(8,128)}) %reduce-scatter.6.cloned.1.call-update) | async-done | bytes 65552 | tf_op jit(solution)/shard_map/reduce_scatter | solution.py:273
  1008.6 648.0 %reduce-scatter.8.cloned.1.call-done = f32[8,1024]{1,0:T(8,128)} async-done(((f32[1024,1024]{1,0:T(8,128)}), f32[8,1024]{1,0:T(8,128)}) %reduce-scatter.8.cloned.1.call-update) | async-done | bytes 32784 | tf_op jit(solution)/shard_map/reduce_scatter | solution.py:273
  1656.7 648.4 %reduce-scatter.4.cloned.1.call-done = f32[8,1024]{1,0:T(8,128)} async-done(((f32[1024,1024]{1,0:T(8,128)}), f32[8,1024]{1,0:T(8,128)}) %reduce-scatter.4.cloned.1.call-update) | async-done | bytes 32784 | tf_op jit(solution)/shard_map/reduce_scatter | solution.py:273
  (231 shorter events, 137.7 us)
Async XLA Ops:
  7.2 12.9 copy-start
  7.2 5.6 copy-start.1
  7.2 1000.6 %reduce-scatter.6.cloned.1.call-start = ((), (), s32[]{:S(2)}) async-start(), calls=%async_computation.4 | async-start | bytes 8454144 | tf_op jit(solution)/shard_map/reduce_scatter | solution.py:273
  12.8 8.0 copy-start.7
  13.1 7.7 copy-start.16
  13.9 6.2 copy-start.9
  13.9 6.9 copy-start.17
  14.8 28.1 %collective-permute-start.5 = (bf16[2,6,16,1024]{3,2,1,0:T(8,128)(2,1)}, bf16[2,6,16,1024]{3,2,1,0:T(8,128)(2,1)}, u32[]{:S(2)}, u32[]{:S(2)}) collective-permute-start(bf16[2,6,16,1024]{3,2,1,0:T(8,128)(2,1)} %get-tuple-element.116), channel_id=1, source_target_pairs={{8,0},{16,8},{24,16},{32,24},{40,32},{48,40},{56,48},{64,56},{72,6... | collective-permute-start | bytes 1179656 | tf_op jit(solution)/shard_map/ppermute | solution.py:26
  16.3 26.7 %collective-permute-start.4 = (bf16[2,6,16,1024]{3,2,1,0:T(8,128)(2,1)}, bf16[2,6,16,1024]{3,2,1,0:T(8,128)(2,1)}, u32[]{:S(2)}, u32[]{:S(2)}) collective-permute-start(bf16[2,6,16,1024]{3,2,1,0:T(8,128)(2,1)} %get-tuple-element.115), channel_id=1, source_target_pairs={{0,8},{8,16},{16,24},{24,32},{32,40},{40,48},{48,56},{56,64},{64,7... | collective-permute-start | bytes 1179656 | tf_op jit(solution)/shard_map/ppermute | solution.py:25
  23.3 38.3 %collective-permute-start.1 = (bf16[2,6,16,1024]{3,2,1,0:T(8,128)(2,1)}, bf16[2,6,16,1024]{3,2,1,0:T(8,128)(2,1)S(1)}, u32[]{:S(2)}, u32[]{:S(2)}) collective-permute-start(bf16[2,6,16,1024]{3,2,1,0:T(8,128)(2,1)} %get-tuple-element.118), channel_id=1, source_target_pairs={{8,0},{16,8},{24,16},{32,24},{40,32},{48,40},{56,48},{64,56},{72,6... | collective-permute-start | bytes 1179656 | tf_op jit(solution)/shard_map/ppermute | solution.py:26
  24.6 37.1 %collective-permute-start = (bf16[2,6,16,1024]{3,2,1,0:T(8,128)(2,1)}, bf16[2,6,16,1024]{3,2,1,0:T(8,128)(2,1)}, u32[]{:S(2)}, u32[]{:S(2)}) collective-permute-start(bf16[2,6,16,1024]{3,2,1,0:T(8,128)(2,1)} %get-tuple-element.117), channel_id=1, source_target_pairs={{0,8},{8,16},{16,24},{24,32},{32,40},{40,48},{48,56},{56,64},{64,7... | collective-permute-start | bytes 1179656 | tf_op jit(solution)/shard_map/ppermute | solution.py:25
  44.6 10.1 copy-start.37
  46.5 27.0 %collective-permute-start.7 = (bf16[2,28,6,1024]{3,0,2,1:T(2,128)(2,1)}, bf16[2,28,6,1024]{3,0,2,1:T(2,128)(2,1)}, u32[]{:S(2)}, u32[]{:S(2)}) collective-permute-start(bf16[2,28,6,1024]{3,0,2,1:T(2,128)(2,1)} %copy.178), channel_id=1, source_target_pairs={{1,0},{2,1},{3,2},{4,3},{5,4},{6,5},{7,6},{9,8},{10,9},{11,10},{12... | collective-permute-start | bytes 2064392 | tf_op jit(solution)/shard_map/ppermute | solution.py:26
  49.4 25.5 %collective-permute-start.6 = (bf16[2,28,6,1024]{3,0,2,1:T(2,128)(2,1)}, bf16[2,28,6,1024]{3,0,2,1:T(2,128)(2,1)}, u32[]{:S(2)}, u32[]{:S(2)}) collective-permute-start(bf16[2,28,6,1024]{3,0,2,1:T(2,128)(2,1)} %copy.177), channel_id=1, source_target_pairs={{0,1},{1,2},{2,3},{3,4},{4,5},{5,6},{6,7},{8,9},{9,10},{10,11},{11... | collective-permute-start | bytes 2064392 | tf_op jit(solution)/shard_map/ppermute | solution.py:25
  63.2 13.0 copy-start.8
  63.2 13.0 copy-start.10
  64.9 21.1 collective-permute-start.3
  67.7 19.8 collective-permute-start.2
  210.6 8.6 copy-start.21
  228.2 10.5 copy-start.35
  239.7 7.7 copy-start.3
  239.7 22.6 collective-permute-start.9
  241.3 21.1 collective-permute-start.8
  254.1 16.3 copy-start.19
  263.3 29.1 %collective-permute-start.11 = (f32[2,28,6,8]{2,3,1,0:T(8,128)}, f32[2,28,6,8]{2,3,1,0:T(8,128)S(1)}, u32[]{:S(2)}, u32[]{:S(2)}) collective-permute-start(f32[2,28,6,8]{2,3,1,0:T(8,128)} %get-tuple-element.122), channel_id=1, source_target_pairs={{1,0},{2,1},{3,2},{4,3},{5,4},{6,5},{7,6},{9,8},{10,9},{11,10},{12... | collective-permute-start | bytes 32264 | tf_op jit(solution)/shard_map/ppermute | solution.py:26
  264.6 27.9 %collective-permute-start.10 = (f32[2,28,6,8]{2,3,1,0:T(8,128)}, f32[2,28,6,8]{2,3,1,0:T(8,128)}, u32[]{:S(2)}, u32[]{:S(2)}) collective-permute-start(f32[2,28,6,8]{2,3,1,0:T(8,128)} %get-tuple-element.121), channel_id=1, source_target_pairs={{0,1},{1,2},{2,3},{3,4},{4,5},{5,6},{6,7},{8,9},{9,10},{10,11},{11... | collective-permute-start | bytes 32264 | tf_op jit(solution)/shard_map/ppermute | solution.py:25
  270.5 6.7 copy-start.2
  284.0 8.5 copy-start.27
  301.7 7.5 copy-start.23
  335.9 1320.8 %reduce-scatter.8.cloned.1.call-start = ((), (), s32[]{:S(2)}) async-start(), calls=%async_computation.5 | async-start | bytes 4227072 | tf_op jit(solution)/shard_map/reduce_scatter | solution.py:273
  352.5 1952.6 %reduce-scatter.4.cloned.1.call-start = ((), (), s32[]{:S(2)}) async-start(), calls=%async_computation.3 | async-start | bytes 4227072 | tf_op jit(solution)/shard_map/reduce_scatter | solution.py:273
  371.7 5.8 copy-start.18
  (29 other events, 68.4 us)
Sparse Core Ops, SparseCore 0:
  336.0 671.7 reduce-scatter.5
  1010.2 646.4 reduce-scatter.7
  1659.0 646.0 reduce-scatter.3

commit v2 on v0

--- a/solution.py
+++ b/solution.py
@@ -268,16 +268,21 @@
     grad_keys = grad_keys.astype(jnp.bfloat16).reshape(tile_rows * tile_cols, model_width)
     grad_values = grad_values.astype(jnp.bfloat16).reshape(tile_rows * tile_cols, model_width)
     contract_dims = (((0,), (0,)), ((), ()))
-    term_list = [
-        lax.dot_general(hidden, grad_query, contract_dims, preferred_element_type=jnp.float32),
-        lax.dot_general(hidden, grad_keys, contract_dims, preferred_element_type=jnp.float32),
-        lax.dot_general(hidden, grad_values, contract_dims, preferred_element_type=jnp.float32),
-        lax.dot_general(
-            attended_rows, grad_flat, contract_dims, preferred_element_type=jnp.float32
-        ),
-    ]
-    weight_grads = lax.psum_scatter(
-        jnp.stack(term_list, axis=1), ("tm", "freq"), scatter_dimension=0, tiled=True
+    hidden_rows = jnp.concatenate([grad_query, grad_keys, grad_values], axis=1)
+    term_rows = jnp.concatenate(
+        [
+            lax.dot_general(hidden, hidden_rows, contract_dims, preferred_element_type=jnp.float32),
+            lax.dot_general(
+                attended_rows, grad_flat, contract_dims, preferred_element_type=jnp.float32
+            ),
+        ],
+        axis=1,
+    )
+    summed = lax.psum(term_rows, ("tm", "freq"))
+    row_count = model_width // (lax.axis_size("tm") * lax.axis_size("freq"))
+    row_start = (lax.axis_index("tm") * lax.axis_size("freq") + lax.axis_index("freq")) * row_count
+    weight_grads = lax.dynamic_slice_in_dim(summed, row_start, row_count, axis=0).reshape(
+        row_count, 4, model_width
     )
     grad_hidden = jnp.dot(grad_query, w_query.T, preferred_element_type=jnp.float32)
     grad_hidden = grad_hidden + jnp.dot(grad_keys, w_key.T, preferred_element_type=jnp.float32)

time: 1080 us -> 606 us (0.56)
  waiting for transfers between devices: 691 us -> 227 us
  local copies, waits for them, and re-layouts: 195 us -> 183 us
    reduce_scatter x1 -> x0, waiting for transfers between devices: 688 us -> none  [local(): lax.psum_scatter(jnp.stack(term_list, axis=1), ('tm', 'freq'), scatter_di...]
    psum x0 -> x1, waiting for transfers between devices: none -> 224 us  [local(): summed = lax.psum(term_rows, ('tm', 'freq'))]
  transfers between devices with their start and end apart: 13 -> 13, of which waited for: 3 -> 3; matrix products, arithmetic and copies ran while one was open for 7% -> 16% of each run, Pallas kernels for 0% -> 0%
where the time goes in v2:
time: 606 us; the launch traced here: 595 us
  waiting for transfers between devices  227 us (37%)
  local copies, waits for them, and re-layouts  183 us (30%)
  matrix products  69.3 us (11%)
  other arithmetic  67.7 us (11%)
  starting transfers between devices  32.4 us (5%)
  between operations  15.3 us (3%)
    psum x1, waiting for transfers between devices, local(): summed = lax.psum(term_rows, ('tm', 'freq'))  224 us
    gather x10, local copies, waits for them, and re-layouts, spread_tiles(): picked = jnp.take(picked, col_index, axis=2)  54 us
    dot_general x7, matrix products, mix(): jnp.einsum(form, left_operand, right_operand, preferred_element_type=jnp....  51.3 us
    squeeze x4, local copies, waits for them, and re-layouts, over_groups(): results = lax.map(lambda group_parts: group_func(*group_parts), grouped)  33.2 us
    transpose x6, local copies, waits for them, and re-layouts, spread_tiles(): picked.transpose(axes_order)  29.2 us
    ppermute x6, starting transfers between devices, extended(): before = lax.ppermute(last, axis, up)  24.2 us
    gather x11, local copies, waits for them, and re-layouts, spread_tiles(): picked = jnp.take(field_map, row_index, axis=0)  22 us
    select_n x3, other arithmetic, spread_tiles(): picked = jnp.take(field_map, row_index, axis=0)  20.1 us
  transfers between devices with their start and end apart: 13, of which 3 were waited for; matrix products, arithmetic and copies ran while one was open for 16% of the time, Pallas kernels for 0%

profile of v2, /device:TPU:0, one launch (start us, length us, event | category | flops | bytes accessed | tf_op | source)
XLA Modules:
  0.0 595.5 jit_solution(6245784730315820183)
XLA Ops:
  21.6 5.7 collective-permute-start
  49.8 4.6 collective-permute-start.2
  64.0 5.6 collective-permute-start.6
  75.8 3.9 gather_fusion.4
  79.7 3.5 collective-permute-done.7
  91.6 3.9 gather_fusion.10
  95.5 3.9 gather_fusion.6
  99.4 3.9 gather_fusion
  103.4 17.8 %broadcast_select_fusion.4 = (bf16[2,20,28,1024]{3,0,2,1:T(2,128)(2,1)}, bf16[2,20,28,1024]{3,0,2,1:T(2,128)(2,1)}, bf16[2,20,28,1024]{3,0,2,1:T(2,128)(2,1)}, bf16[2,20,28,1024]{3,0,2,1:T(2,128)(2,1)}) fusion(pred[2,20]{0,1:T(8,128)(4,1)S(1)} %copy.149, bf16[2,20,28,1024]{3,2,1,0:T(8,128)(2,1)} %bitcast.178, bf16[2,20,28,1024]{3,2,1,0:T(8,128)(2,1)} %bitcast.177, ...), kind=kLoop, calls=%fused_computation.19 | loop fusion | flops 4587520 | bytes 18350120 | tf_op jit(solution)/shard_map/jit(_take)/select_n | solution.py:75
  121.1 11.7 %gather_fusion.11 = bf16[40,2,20,1024]{3,1,2,0:T(2,128)(2,1)} fusion(bf16[2,20,28,1024]{3,0,2,1:T(2,128)(2,1)} %get-tuple-element.110, s32[1024]{0:T(1024)S(1)} %copy-done.31), kind=kCustom, calls=%fused_computation.11.clone | custom fusion | bytes 6553760 | tf_op jit(solution)/shard_map/jit(_take)/gather | solution.py:76
  132.9 11.9 %gather_fusion.5 = bf16[40,2,20,1024]{3,1,2,0:T(2,128)(2,1)} fusion(bf16[2,20,28,1024]{3,0,2,1:T(2,128)(2,1)} %get-tuple-element.111, s32[1024]{0:T(1024)S(1)} %copy-done.31), kind=kCustom, calls=%fused_computation.9.clone | custom fusion | bytes 6553760 | tf_op jit(solution)/shard_map/jit(_take)/gather | solution.py:76
  144.8 11.7 %gather_fusion.7 = bf16[40,2,20,1024]{3,1,2,0:T(2,128)(2,1)} fusion(bf16[2,20,28,1024]{3,0,2,1:T(2,128)(2,1)} %get-tuple-element.112, s32[1024]{0:T(1024)S(1)} %copy-done.31), kind=kCustom, calls=%fused_computation.10.clone | custom fusion | bytes 6553760 | tf_op jit(solution)/shard_map/jit(_take)/gather | solution.py:76
  156.6 11.8 %gather_fusion.1 = bf16[40,2,20,1024]{3,1,2,0:T(2,128)(2,1)} fusion(bf16[2,20,28,1024]{3,0,2,1:T(2,128)(2,1)} %get-tuple-element.113, s32[1024]{0:T(1024)S(1)} %copy-done.31), kind=kCustom, calls=%fused_computation.1.clone | custom fusion | bytes 6553760 | tf_op jit(solution)/shard_map/jit(_take)/gather | solution.py:76
  168.3 16.0 %fusion.3 = (bf16[2,2,20,20,1024]{4,0,2,3,1:T(2,128)(2,1)}, bf16[2,2,20,20,1024]{4,0,2,3,1:T(2,128)(2,1)S(1)}, bf16[2,2,20,20,1024]{4,0,2,3,1:T(2,128)(2,1)}, bf16[2,2,20,20,1024]{4,0,2,3,1:T(2,128)(2,1)}) fusion(bf16[2,20,2,20,1024]{4,2,3,1,0:T(2,128)(2,1)} %bitcast.172, pred[2,20]{1,0:T(4,128)(4,1)S(1)} %copy-done.33, ...), kind=kLoop, calls=%fused_computation.35 | loop fusion | flops 6553600 | bytes 26214440 | tf_op jit(solution)/shard_map/transpose | solution.py:78
  184.3 6.7 %copy.164 = bf16[2,2,20,20,1024]{4,1,0,3,2:T(2,128)(2,1)} copy(bf16[2,2,20,20,1024]{4,0,2,3,1:T(2,128)(2,1)S(1)} %get-tuple-element.115) | data formatting | bytes 6553600 | tf_op jit(solution)/shard_map/transpose | solution.py:78
  191.0 8.2 %squeeze.76 = bf16[4,400,8,128]{3,2,0,1:T(8,128)(2,1)} reshape(bf16[2,2,20,20,1024]{4,1,0,3,2:T(2,128)(2,1)} %copy.164) | data formatting | bytes 6553600 | tf_op jit(solution)/shard_map/while/body/jit(dynamic_index_in_dim)/squeeze | solution.py:100
  199.2 8.7 %copy.156 = bf16[2,2,20,20,1024]{4,1,0,3,2:T(2,128)(2,1)} copy(bf16[2,2,20,20,1024]{4,0,2,3,1:T(2,128)(2,1)} %get-tuple-element.117) | data formatting | bytes 6553600 | tf_op jit(solution)/shard_map/transpose | solution.py:78
  207.9 8.4 %squeeze.73 = bf16[4,400,8,128]{3,2,0,1:T(8,128)(2,1)} reshape(bf16[2,2,20,20,1024]{4,1,0,3,2:T(2,128)(2,1)} %copy.156) | data formatting | bytes 6553600 | tf_op jit(solution)/shard_map/while/body/jit(dynamic_index_in_dim)/squeeze | solution.py:100
  216.4 5.4 fusion.4
  225.5 6.8 %fusion.74 = bf16[4,64,8,128]{3,1,2,0:T(8,128)(2,1)S(1)} fusion(bf16[4,400,8,128]{3,2,0,1:T(8,128)(2,1)} %squeeze.73, f32[4,8,64]{2,1,0:T(8,128)S(1)} %log_add_fusion, f32[4,8,64,400]{3,2,1,0:T(8,128)} %copy-done.12, pred[4,64,400]{2,1,0:T(8,128)(4,1)S(1)} %copy-done.23), kind=kOutput, calls=%fused_computation.93 | convolution fusion | flops 214073344 | bytes 7188480 | tf_op jit(solution)/shard_map/while/body/eval_jaxpr/nhqk,nkhd->nqhd/dot_general | solution.py:32
  233.8 9.9 %multiply_reduce_fusion = (f32[4,8,64]{2,1,0:T(8,128)S(1)}, f32[4,8,64,400]{3,2,1,0:T(8,128)}) fusion(f32[4,8,64]{2,1,0:T(8,128)S(1)} %log_add_fusion, f32[4,8,64,400]{3,2,1,0:T(8,128)} %copy-done.12, pred[4,64,400]{2,1,0:T(8,128)(4,1)S(1)} %copy-done.23, bf16[4,400,8,128]{3,2,0,1:T(8,128)(2,1)} %squeeze.73, bf16[4,64,8,128]{3,2,1,0:T(8,128)(2,1)} %bitcast.219), kind=kOutput, calls=%fused_computation.26 | convolution fusion | flops 214628352 | bytes 10473472 | tf_op jit(solution)/shard_map/while/body/eval_jaxpr/nqhd,nkhd->nhqk/dot_general | solution.py:32
  257.3 4.6 fusion.79
  261.8 6.8 %copy.183 = bf16[2,2,20,20,1024]{4,1,0,3,2:T(2,128)(2,1)} copy(bf16[2,2,20,20,1024]{4,0,2,3,1:T(2,128)(2,1)S(1)} %copy-done.3) | data formatting | bytes 6553600 | tf_op jit(solution)/shard_map/transpose | solution.py:78
  268.6 8.3 %squeeze.79 = bf16[4,400,8,128]{3,2,0,1:T(8,128)(2,1)} reshape(bf16[2,2,20,20,1024]{4,1,0,3,2:T(2,128)(2,1)} %copy.183) | data formatting | bytes 6553600 | tf_op jit(solution)/shard_map/while/body/jit(dynamic_index_in_dim)/squeeze | solution.py:100
  277.8 4.8 collective-permute-start.10
  284.2 6.7 %fusion.6 = f32[4,8,64,400]{3,2,1,0:T(8,128)} fusion(bf16[4,400,8,128]{3,2,0,1:T(8,128)(2,1)} %squeeze.79, bf16[4,64,8,128]{3,2,1,0:T(8,128)(2,1)S(1)} %bitcast.215), kind=kOutput, calls=%fused_computation.38 | convolution fusion | flops 209715200 | bytes 7077888 | tf_op jit(solution)/shard_map/while/body/eval_jaxpr/nkhd,nqhd->nhkq/dot_general | solution.py:32
  290.9 6.7 %copy.196 = bf16[2,2,20,20,1024]{4,1,0,3,2:T(2,128)(2,1)} copy(bf16[2,2,20,20,1024]{4,0,2,3,1:T(2,128)(2,1)S(1)} %copy-done.2) | data formatting | bytes 6553600 | tf_op jit(solution)/shard_map/transpose | solution.py:78
  297.7 8.3 %squeeze.84 = bf16[4,400,8,128]{3,2,0,1:T(8,128)(2,1)} reshape(bf16[2,2,20,20,1024]{4,1,0,3,2:T(2,128)(2,1)} %copy.196) | data formatting | bytes 6553600 | tf_op jit(solution)/shard_map/while/body/jit(dynamic_index_in_dim)/squeeze | solution.py:100
  318.3 6.6 %fusion.69 = bf16[4,64,8,128]{3,1,2,0:T(8,128)(2,1)S(1)} fusion(bf16[4,400,8,128]{3,2,0,1:T(8,128)(2,1)} %squeeze.84, f32[4,8,64,400]{3,2,1,0:T(8,128)} %fusion.6, f32[4,8,400]{2,1,0:T(8,128)S(1)} %bitcast.226, pred[64,400]{1,0:T(8,128)(4,1)S(1)} %copy-done.30), kind=kOutput, calls=%fused_computation.92 | convolution fusion | flops 213254144 | bytes 7154688 | tf_op jit(solution)/shard_map/while/body/eval_jaxpr/nhkq,nqhd->nkhd/dot_general | solution.py:32
  327.4 11.4 %fusion.64 = bf16[4,64,8,128]{3,1,2,0:T(8,128)(2,1)} fusion(bf16[4,400,8,128]{3,2,0,1:T(8,128)(2,1)} %squeeze.79, f32[4,8,64,400]{3,2,1,0:T(8,128)} %fusion.6, f32[4,8,400]{2,1,0:T(8,128)S(1)} %bitcast.228, f32[4,8,400]{2,1,0:T(8,128)S(1)} %bitcast.227, pred[64,400]{1,0:T(8,128)(4,1)S(1)} %copy-done.30, bf16[4,400,8,128]{3,2,0,1:T(8,128)(2,1)} %squeeze.84, ...), kind=kOutput, calls=%fused_computation.91 | convolution fusion | flops 425426944 | bytes 11006976 | tf_op jit(solution)/shard_map/while/body/eval_jaxpr/nhkq,nqhd->nkhd/dot_general | solution.py:32
  348.0 6.1 %pad_maximum_fusion = f32[1024,4096]{1,0:T(8,128)} fusion(f32[1024,1024]{1,0:T(8,128)S(1)} %copy-done.14, f32[1024,3072]{1,0:T(8,128)S(1)} %fusion.39), kind=kLoop, calls=%fused_computation.14 | loop fusion | flops 4194304 | bytes 33554432 | tf_op jit(solution)/shard_map/concatenate | solution.py:272
  363.1 223.6 %all-reduce.2.cloned.1.call-done = f32[1024,4096]{1,0:T(8,128)} async-done(((f32[1024,4096]{1,0:T(8,128)}), f32[1024,4096]{1,0:T(8,128)}) %all-reduce.2.cloned.1.call-update) | async-done | bytes 16777232 | tf_op jit(solution)/shard_map/psum | solution.py:281
  (219 shorter events, 116.5 us)
Async XLA Ops:
  7.2 11.8 %copy-start = (bf16[1024,1024]{1,0:T(8,128)(2,1)S(1)}, bf16[1024,1024]{1,0:T(8,128)(2,1)}, u32[]{:S(2)}) copy-start(bf16[1024,1024]{1,0:T(8,128)(2,1)} %param.21) | copy-start | bytes 6291460
  7.2 579.5 %all-reduce.2.cloned.1.call-start = ((), (), s32[]{:S(2)}) async-start(), calls=%async_computation | async-start | bytes 33554432 | tf_op jit(solution)/shard_map/psum | solution.py:281
  12.1 7.6 %copy-start.16 = (bf16[256,1024]{1,0:T(8,128)(2,1)}, bf16[256,1024]{1,0:T(8,128)(2,1)S(1)}, u32[]{:S(2)}) copy-start(bf16[256,1024]{1,0:T(8,128)(2,1)S(1)} %fusion.83) | copy-start | bytes 1572868
  16.4 41.6 %collective-permute-start.4 = (bf16[2,6,16,1024]{3,2,1,0:T(8,128)(2,1)}, bf16[2,6,16,1024]{3,2,1,0:T(8,128)(2,1)S(1)}, u32[]{:S(2)}, u32[]{:S(2)}) collective-permute-start(bf16[2,6,16,1024]{3,2,1,0:T(8,128)(2,1)} %get-tuple-element.90), channel_id=1, source_target_pairs={{0,8},{8,16},{16,24},{24,32},{32,40},{40,48},{48,56},{56,64},{64,7... | collective-permute-start | bytes 1179656 | tf_op jit(solution)/shard_map/ppermute | solution.py:25
  17.7 40.3 %collective-permute-start.5 = (bf16[2,6,16,1024]{3,2,1,0:T(8,128)(2,1)}, bf16[2,6,16,1024]{3,2,1,0:T(8,128)(2,1)}, u32[]{:S(2)}, u32[]{:S(2)}) collective-permute-start(bf16[2,6,16,1024]{3,2,1,0:T(8,128)(2,1)} %get-tuple-element.91), channel_id=1, source_target_pairs={{8,0},{16,8},{24,16},{32,24},{40,32},{48,40},{56,48},{64,56},{72,6... | collective-permute-start | bytes 1179656 | tf_op jit(solution)/shard_map/ppermute | solution.py:26
  21.6 23.4 %collective-permute-start = (bf16[2,6,16,1024]{3,2,1,0:T(8,128)(2,1)}, bf16[2,6,16,1024]{3,2,1,0:T(8,128)(2,1)}, u32[]{:S(2)}, u32[]{:S(2)}) collective-permute-start(bf16[2,6,16,1024]{3,2,1,0:T(8,128)(2,1)} %get-tuple-element.92), channel_id=1, source_target_pairs={{0,8},{8,16},{16,24},{24,32},{32,40},{40,48},{48,56},{56,64},{64,7... | collective-permute-start | bytes 1179656 | tf_op jit(solution)/shard_map/ppermute | solution.py:25
  27.2 17.8 %collective-permute-start.1 = (bf16[2,6,16,1024]{3,2,1,0:T(8,128)(2,1)}, bf16[2,6,16,1024]{3,2,1,0:T(8,128)(2,1)}, u32[]{:S(2)}, u32[]{:S(2)}) collective-permute-start(bf16[2,6,16,1024]{3,2,1,0:T(8,128)(2,1)} %get-tuple-element.93), channel_id=1, source_target_pairs={{8,0},{16,8},{24,16},{32,24},{40,32},{48,40},{56,48},{64,56},{72,6... | collective-permute-start | bytes 1179656 | tf_op jit(solution)/shard_map/ppermute | solution.py:26
  45.0 12.3 %copy-start.29 = (pred[64,400]{1,0:T(8,128)(4,1)}, pred[64,400]{1,0:T(8,128)(4,1)S(1)}, u32[]{:S(2)}) copy-start(pred[64,400]{1,0:T(8,128)(4,1)S(1)} %fusion.91) | copy-start | bytes 76804
  46.7 7.7 %copy-start.7 = (bf16[256,1024]{1,0:T(8,128)(2,1)S(1)}, bf16[256,1024]{1,0:T(8,128)(2,1)}, u32[]{:S(2)}) copy-start(bf16[256,1024]{1,0:T(8,128)(2,1)} %copy-done.6) | copy-start | bytes 1572868
  47.0 8.3 %copy-start.5 = (bf16[256,1024]{1,0:T(8,128)(2,1)S(1)}, bf16[256,1024]{1,0:T(8,128)(2,1)}, u32[]{:S(2)}) copy-start(bf16[256,1024]{1,0:T(8,128)(2,1)} %copy-done.4) | copy-start | bytes 1572868
  48.5 8.8 %copy-start.41 = (pred[4,400]{1,0:T(4,128)(4,1)S(1)}, pred[4,400]{1,0:T(4,128)(4,1)}, u32[]{:S(2)}) copy-start(pred[4,400]{1,0:T(4,128)(4,1)} %gt.19) | copy-start | bytes 4804
  48.5 21.1 %collective-permute-start.3 = (bf16[2,28,6,1024]{3,0,2,1:T(2,128)(2,1)S(1)}, bf16[2,28,6,1024]{3,0,2,1:T(2,128)(2,1)S(1)}, u32[]{:S(2)}, u32[]{:S(2)}) collective-permute-start(bf16[2,28,6,1024]{3,0,2,1:T(2,128)(2,1)S(1)} %copy.151), channel_id=1, source_target_pairs={{1,0},{2,1},{3,2},{4,3},{5,4},{6,5},{7,6},{9,8},{10,9},{11,10},{12... | collective-permute-start | bytes 2064392 | tf_op jit(solution)/shard_map/ppermute | solution.py:26
  49.8 20.0 %collective-permute-start.2 = (bf16[2,28,6,1024]{3,0,2,1:T(2,128)(2,1)S(1)}, bf16[2,28,6,1024]{3,0,2,1:T(2,128)(2,1)S(1)}, u32[]{:S(2)}, u32[]{:S(2)}) collective-permute-start(bf16[2,28,6,1024]{3,0,2,1:T(2,128)(2,1)S(1)} %copy.150), channel_id=1, source_target_pairs={{0,1},{1,2},{2,3},{3,4},{4,5},{5,6},{6,7},{8,9},{9,10},{10,11},{11... | collective-permute-start | bytes 2064392 | tf_op jit(solution)/shard_map/ppermute | solution.py:25
  62.7 20.5 %collective-permute-start.7 = (bf16[2,28,6,1024]{3,0,2,1:T(2,128)(2,1)}, bf16[2,28,6,1024]{3,0,2,1:T(2,128)(2,1)}, u32[]{:S(2)}, u32[]{:S(2)}) collective-permute-start(bf16[2,28,6,1024]{3,0,2,1:T(2,128)(2,1)} %copy.178), channel_id=1, source_target_pairs={{1,0},{2,1},{3,2},{4,3},{5,4},{6,5},{7,6},{9,8},{10,9},{11,10},{12... | collective-permute-start | bytes 2064392 | tf_op jit(solution)/shard_map/ppermute | solution.py:26
  64.0 20.7 %collective-permute-start.6 = (bf16[2,28,6,1024]{3,0,2,1:T(2,128)(2,1)}, bf16[2,28,6,1024]{3,0,2,1:T(2,128)(2,1)}, u32[]{:S(2)}, u32[]{:S(2)}) collective-permute-start(bf16[2,28,6,1024]{3,0,2,1:T(2,128)(2,1)} %copy.177), channel_id=1, source_target_pairs={{0,1},{1,2},{2,3},{3,4},{4,5},{5,6},{6,7},{8,9},{9,10},{10,11},{11... | collective-permute-start | bytes 2064392 | tf_op jit(solution)/shard_map/ppermute | solution.py:25
  156.6 11.8 %copy-start.33 = (pred[2,20]{1,0:T(4,128)(4,1)S(1)}, pred[2,20]{1,0:T(4,128)(4,1)}, u32[]{:S(2)}) copy-start(pred[2,20]{1,0:T(4,128)(4,1)} %compare_and_fusion) | copy-start | bytes 124
  207.9 8.4 %copy-start.23 = (pred[4,64,400]{2,1,0:T(8,128)(4,1)S(1)}, pred[4,64,400]{2,1,0:T(8,128)(4,1)}, u32[]{:S(2)}) copy-start(pred[4,64,400]{2,1,0:T(8,128)(4,1)} %broadcast_and_fusion) | copy-start | bytes 307204
  207.9 8.4 %copy-start.26 = (bf16[32,8,8,128]{3,2,1,0:T(8,128)(2,1)S(1)}, bf16[32,8,8,128]{3,2,1,0:T(8,128)(2,1)}, u32[]{:S(2)}) copy-start(bf16[32,8,8,128]{3,2,1,0:T(8,128)(2,1)} %copy.223) | copy-start | bytes 1572868
  233.8 17.6 %copy-start.21 = (bf16[16,16,1024]{2,1,0:T(8,128)(2,1)S(1)}, bf16[16,16,1024]{2,1,0:T(8,128)(2,1)}, u32[]{:S(2)}) copy-start(bf16[16,16,1024]{2,1,0:T(8,128)(2,1)} %param.23) | copy-start | bytes 1572868
  233.8 17.6 %copy-start.24 = (bf16[2,8,2,8,1024]{4,3,2,1,0:T(8,128)(2,1)S(1)}, bf16[2,8,2,8,1024]{4,3,2,1,0:T(8,128)(2,1)}, u32[]{:S(2)}) copy-start(bf16[2,8,2,8,1024]{4,3,2,1,0:T(8,128)(2,1)} %copy.169) | copy-start | bytes 1572868
  247.7 29.2 %collective-permute-start.8 = (f32[2,6,16,8]{2,3,1,0:T(8,128)}, f32[2,6,16,8]{2,3,1,0:T(8,128)S(1)}, u32[]{:S(2)}, u32[]{:S(2)}) collective-permute-start(f32[2,6,16,8]{2,3,1,0:T(8,128)} %get-tuple-element.108), channel_id=1, source_target_pairs={{0,8},{8,16},{16,24},{24,32},{32,40},{40,48},{48,56},{56,64},{64,7... | collective-permute-start | bytes 18440 | tf_op jit(solution)/shard_map/ppermute | solution.py:25
  250.0 26.9 %collective-permute-start.9 = (f32[2,6,16,8]{2,3,1,0:T(8,128)}, f32[2,6,16,8]{2,3,1,0:T(8,128)S(1)}, u32[]{:S(2)}, u32[]{:S(2)}) collective-permute-start(f32[2,6,16,8]{2,3,1,0:T(8,128)} %get-tuple-element.109), channel_id=1, source_target_pairs={{8,0},{16,8},{24,16},{32,24},{40,32},{48,40},{56,48},{64,56},{72,6... | collective-permute-start | bytes 18440 | tf_op jit(solution)/shard_map/ppermute | solution.py:26
  251.4 5.9 copy-start.43
  268.6 15.6 %copy-start.19 = (bf16[32,8,8,128]{3,2,1,0:T(8,128)(2,1)S(1)}, bf16[32,8,8,128]{3,2,1,0:T(8,128)(2,1)}, u32[]{:S(2)}) copy-start(bf16[32,8,8,128]{3,2,1,0:T(8,128)(2,1)} %copy.225) | copy-start | bytes 1572868
  276.9 14.0 %copy-start.27 = (f32[2,6,16,8]{2,3,1,0:T(8,128)}, f32[2,6,16,8]{2,3,1,0:T(8,128)S(1)}, u32[]{:S(2)}) copy-start(f32[2,6,16,8]{2,3,1,0:T(8,128)S(1)} %collective-permute-done.8) | copy-start | bytes 18436
  276.9 14.0 %copy-start.28 = (f32[2,6,16,8]{2,3,1,0:T(8,128)}, f32[2,6,16,8]{2,3,1,0:T(8,128)S(1)}, u32[]{:S(2)}) copy-start(f32[2,6,16,8]{2,3,1,0:T(8,128)S(1)} %collective-permute-done.9) | copy-start | bytes 18436
  277.8 30.7 %collective-permute-start.10 = (f32[2,28,6,8]{2,3,1,0:T(8,128)}, f32[2,28,6,8]{2,3,1,0:T(8,128)}, u32[]{:S(2)}, u32[]{:S(2)}) collective-permute-start(f32[2,28,6,8]{2,3,1,0:T(8,128)} %get-tuple-element.96), channel_id=1, source_target_pairs={{0,1},{1,2},{2,3},{3,4},{4,5},{5,6},{6,7},{8,9},{9,10},{10,11},{11... | collective-permute-start | bytes 32264 | tf_op jit(solution)/shard_map/ppermute | solution.py:25
  282.5 26.0 %collective-permute-start.11 = (f32[2,28,6,8]{2,3,1,0:T(8,128)}, f32[2,28,6,8]{2,3,1,0:T(8,128)}, u32[]{:S(2)}, u32[]{:S(2)}) collective-permute-start(f32[2,28,6,8]{2,3,1,0:T(8,128)} %get-tuple-element.97), channel_id=1, source_target_pairs={{1,0},{2,1},{3,2},{4,3},{5,4},{6,5},{7,6},{9,8},{10,9},{11,10},{12... | collective-permute-start | bytes 32264 | tf_op jit(solution)/shard_map/ppermute | solution.py:26
  284.2 6.7 %copy-start.2 = (bf16[2,2,20,20,1024]{4,0,2,3,1:T(2,128)(2,1)S(1)}, bf16[2,2,20,20,1024]{4,0,2,3,1:T(2,128)(2,1)}, u32[]{:S(2)}) copy-start(bf16[2,2,20,20,1024]{4,0,2,3,1:T(2,128)(2,1)} %get-tuple-element.114) | copy-start | bytes 9830404
  306.4 5.8 copy-start.34
  327.4 16.8 %copy-start.8 = (bf16[2,8,2,8,1024]{4,3,2,1,0:T(8,128)(2,1)}, bf16[2,8,2,8,1024]{4,3,2,1,0:T(8,128)(2,1)S(1)}, u32[]{:S(2)}) copy-start(bf16[2,8,2,8,1024]{4,3,2,1,0:T(8,128)(2,1)S(1)} %copy.207) | copy-start | bytes 1572868
  354.1 5.7 copy-start.11
  (25 other events, 65.0 us)
Sparse Core Ops, SparseCore 0:
  354.2 232.4 all-reduce.1

commit v3 on v2

v3 whole, which is shorter than its diff:
```python
import math

import jax
import jax.numpy as jnp
from jax import lax
from jax.sharding import PartitionSpec as P

HEADS = 8


window_reach = 6
tile_edge = 8
span_edge = 20
norm_eps = 1e-05
far_value = -1e30


def extended(array, sides, width):
    for axis, dim in sides:
        size, length = (lax.axis_size(axis), array.shape[dim])
        up = [(i, (i + 1) % size) for i in range(size - 1)]
        down = [(j, i) for i, j in up]
        last = lax.slice_in_dim(array, length - width, length, axis=dim)
        leading = lax.slice_in_dim(array, 0, width, axis=dim)
        before = lax.ppermute(last, axis, up)
        after = lax.ppermute(leading, axis, down)
        array = jnp.concatenate([before, array, after], axis=dim)
    return array


def mix(form, left_operand, right_operand):
    return jnp.einsum(form, left_operand, right_operand, preferred_element_type=jnp.float32)


def window_mask():
    query_pos = jnp.arange(tile_edge * tile_edge)
    key_pos = jnp.arange(span_edge * span_edge)
    rise_rows = (key_pos // span_edge)[None, :] - (query_pos // tile_edge)[:, None]
    rise_cols = (key_pos % span_edge)[None, :] - (query_pos % tile_edge)[:, None]
    return (
        (rise_rows >= 0)
        & (rise_rows <= 2 * window_reach)
        & (rise_cols >= 0)
        & (rise_cols <= 2 * window_reach)
    )


def pack_tiles(field_map):
    lead, row_total, col_total = field_map.shape[:3]
    trailing = field_map.shape[3:]
    shaped = field_map.reshape(
        (lead, row_total // tile_edge, tile_edge, col_total // tile_edge, tile_edge) + trailing
    )
    axes_order = (0, 1, 3, 2, 4) + tuple(range(5, shaped.ndim))
    return shaped.transpose(axes_order).reshape(
        (lead, row_total // tile_edge * (col_total // tile_edge), tile_edge * tile_edge)
        + trailing
    )


def unpack_tiles(tile_stack, row_total, col_total):
    lead = tile_stack.shape[0]
    trailing = tile_stack.shape[3:]
    shaped = tile_stack.reshape(
        (lead, row_total // tile_edge, col_total // tile_edge, tile_edge, tile_edge) + trailing
    )
    axes_order = (0, 1, 3, 2, 4) + tuple(range(5, shaped.ndim))
    return shaped.transpose(axes_order).reshape((lead, row_total, col_total) + trailing)


def spread_tiles(field_map, row_total, col_total):
    lead = field_map.shape[0]
    trailing = field_map.shape[3:]
    spans = []
    for tile_row in range(row_total // tile_edge):
        for tile_col in range(col_total // tile_edge):
            row_at, col_at = tile_row * tile_edge, tile_col * tile_edge
            spans.append(
                field_map[:, row_at : row_at + span_edge, col_at : col_at + span_edge].reshape(
                    (lead, span_edge * span_edge) + trailing
                )
            )
    return jnp.stack(spans, axis=1)


def attend_both(q_heads, k_rim, v_rim, g_heads, key_ok, head_count):
    head_count, row_total, col_total, head_dim = q_heads.shape
    score_scale = 1.0 / math.sqrt(head_dim)
    inside = window_mask()
    q_part = pack_tiles(q_heads)
    g_part = pack_tiles(g_heads)
    k_part = spread_tiles(k_rim, row_total, col_total)
    v_part = spread_tiles(v_rim, row_total, col_total)
    ok_part = spread_tiles(key_ok[None], row_total, col_total)[0]
    allowed = inside[None, None] & (ok_part[None, :, None, :] > 0.5)
    scores = mix("hnqd,hnkd->hnqk", q_part, k_part) * score_scale
    scores = jnp.where(allowed, scores, far_value)
    row_max = jnp.max(scores, axis=-1, keepdims=True)
    log_total = row_max + jnp.log(jnp.sum(jnp.exp(scores - row_max), axis=-1, keepdims=True))
    soft_weights = jnp.where(allowed, jnp.exp(scores - log_total), 0.0)
    attended = mix("hnqk,hnkd->hnqd", soft_weights.astype(jnp.bfloat16), v_part)
    grad_probs = mix("hnqd,hnkd->hnqk", g_part, v_part)
    spread = jnp.sum(soft_weights * grad_probs, axis=-1, keepdims=True)
    grad_scores = (soft_weights * (grad_probs - spread) * score_scale).astype(jnp.bfloat16)
    grad_query = mix("hnqk,hnkd->hnqd", grad_scores, k_part)
    return (
        unpack_tiles(attended.astype(jnp.bfloat16), row_total, col_total),
        unpack_tiles(grad_query.astype(jnp.bfloat16), row_total, col_total),
        unpack_tiles(log_total[..., 0], row_total, col_total),
        unpack_tiles(spread[..., 0], row_total, col_total),
    )


def attend_key_grad(k_heads, v_heads, q_rim, g_rim, log_rim, spread_rim, head_count):
    head_count, row_total, col_total, head_dim = k_heads.shape
    score_scale = 1.0 / math.sqrt(head_dim)
    inside = window_mask()
    k_part = pack_tiles(k_heads)
    v_part = pack_tiles(v_heads)
    q_part = spread_tiles(q_rim, row_total, col_total)
    g_part = spread_tiles(g_rim, row_total, col_total)
    l_part = spread_tiles(log_rim, row_total, col_total)
    s_part = spread_tiles(spread_rim, row_total, col_total)
    scores = mix("hnkd,hnqd->hnkq", k_part, q_part) * score_scale
    soft_weights = jnp.where(inside[None, None], jnp.exp(scores - l_part[:, :, None, :]), 0.0)
    grad_probs = mix("hnkd,hnqd->hnkq", v_part, g_part)
    grad_scores = (soft_weights * (grad_probs - s_part[:, :, None, :]) * score_scale).astype(
        jnp.bfloat16
    )
    grad_keys = mix("hnkq,hnqd->hnkd", grad_scores, q_part)
    grad_values = mix("hnkq,hnqd->hnkd", soft_weights.astype(jnp.bfloat16), g_part)
    return (
        unpack_tiles(grad_keys.astype(jnp.bfloat16), row_total, col_total),
        unpack_tiles(grad_values.astype(jnp.bfloat16), row_total, col_total),
    )


def layer_norm(flat_rows):
    wide_values = flat_rows.astype(jnp.float32)
    center = jnp.mean(wide_values, axis=-1, keepdims=True)
    shifted = wide_values - center
    inverse = lax.rsqrt(jnp.mean(shifted * shifted, axis=-1, keepdims=True) + norm_eps)
    return (shifted * inverse, inverse)


def local(tokens, w_query, w_key, w_value, w_out, d_out):
    tile_rows, tile_cols, model_width = tokens.shape
    head_dim = model_width // HEADS
    token_count = tile_rows * tile_cols
    flat_rows = tokens.reshape(token_count, model_width)
    normed, inverse = layer_norm(flat_rows)
    hidden = normed.astype(jnp.bfloat16)

    def split_heads(weight):
        return weight.reshape(model_width, HEADS, head_dim)

    def project(weight):
        rows = mix("td,dhe->hte", hidden, split_heads(weight)).astype(jnp.bfloat16)
        return rows.reshape(HEADS, tile_rows, tile_cols, head_dim)

    q_heads = project(w_query)
    k_heads = project(w_key)
    v_heads = project(w_value)
    grad_flat = d_out.reshape(token_count, model_width)
    out_heads = w_out.reshape(HEADS, head_dim, model_width)
    g_heads = mix("tf,hef->hte", grad_flat, out_heads).astype(jnp.bfloat16)
    g_heads = g_heads.reshape(HEADS, tile_rows, tile_cols, head_dim)
    time_all = tile_rows * lax.axis_size("tm")
    freq_all = tile_cols * lax.axis_size("freq")
    time_start = lax.axis_index("tm") * tile_rows
    freq_start = lax.axis_index("freq") * tile_cols

    def inside_map(margin):
        time_pos = time_start - margin + jnp.arange(tile_rows + 2 * margin)
        freq_pos = freq_start - margin + jnp.arange(tile_cols + 2 * margin)
        time_ok = (time_pos >= 0) & (time_pos < time_all)
        freq_ok = (freq_pos >= 0) & (freq_pos < freq_all)
        return (time_ok[:, None] & freq_ok[None, :]).astype(jnp.float32)

    sides = (("tm", 2), ("freq", 3))
    near_rim = extended(jnp.stack([k_heads, v_heads]), sides, window_reach)
    beside_all = extended(jnp.stack([q_heads, g_heads]), sides, window_reach)
    attended, grad_query, log_own, spread_own = attend_both(
        q_heads, near_rim[0], near_rim[1], g_heads, inside_map(window_reach), HEADS
    )
    stats_rim = extended(jnp.stack([log_own, spread_own]), sides, window_reach)
    grad_keys, grad_values = attend_key_grad(
        k_heads, v_heads, beside_all[0], beside_all[1], stats_rim[0], stats_rim[1], HEADS
    )
    attended = attended.reshape(HEADS, token_count, head_dim)
    grad_query = grad_query.reshape(HEADS, token_count, head_dim)
    grad_keys = grad_keys.reshape(HEADS, token_count, head_dim)
    grad_values = grad_values.reshape(HEADS, token_count, head_dim)
    output = (flat_rows.astype(jnp.float32) + mix("hte,hef->tf", attended, out_heads)).astype(
        jnp.bfloat16
    )

    def weight_term(grad_heads):
        return mix("td,hte->dhe", hidden, grad_heads).reshape(model_width, model_width)

    term_rows = jnp.concatenate(
        [
            weight_term(grad_query),
            weight_term(grad_keys),
            weight_term(grad_values),
            mix("hte,tf->hef", attended, grad_flat).reshape(model_width, model_width),
        ],
        axis=1,
    )
    summed = lax.psum(term_rows, ("tm", "freq"))
    row_count = model_width // (lax.axis_size("tm") * lax.axis_size("freq"))
    row_start = (lax.axis_index("tm") * lax.axis_size("freq") + lax.axis_index("freq")) * row_count
    weight_grads = lax.dynamic_slice_in_dim(summed, row_start, row_count, axis=0).reshape(
        row_count, 4, model_width
    )
    grad_hidden = mix("hte,dhe->td", grad_query, split_heads(w_query))
    grad_hidden = grad_hidden + mix("hte,dhe->td", grad_keys, split_heads(w_key))
    grad_hidden = grad_hidden + mix("hte,dhe->td", grad_values, split_heads(w_value))
    center_grad = jnp.mean(grad_hidden, axis=-1, keepdims=True)
    along = jnp.mean(grad_hidden * normed, axis=-1, keepdims=True)
    input_grad = (
        grad_flat.astype(jnp.float32) + (grad_hidden - center_grad - normed * along) * inverse
    ).astype(jnp.bfloat16)
    return (
        output.reshape(tile_rows, tile_cols, model_width),
        input_grad.reshape(tile_rows, tile_cols, model_width),
        weight_grads,
    )


def solution(mesh):
    in_specs = (P("tm", "freq", None), P(), P(), P(), P(), P("tm", "freq", None))
    out_specs = (P("tm", "freq", None), P("tm", "freq", None), P(("tm", "freq"), None, None))
    return jax.shard_map(local, mesh=mesh, in_specs=in_specs, out_specs=out_specs, check_vma=False)
```

time: 606 us -> 439 us (0.72)
  local copies, waits for them, and re-layouts: 183 us -> 61.1 us
  other arithmetic: 67.7 us -> 25 us
  matrix products: 69.3 us -> 50.4 us
  waiting for transfers between devices: 227 us -> 243 us
    gather x21 -> x0, local copies, waits for them, and re-layouts: 76 us -> none  [the longest x10 54 us: spread_tiles(): picked = jnp.take(picked, col_index, axis=2)]
    squeeze x5 -> x1, local copies, waits for them, and re-layouts: 33.2 us -> 0.02 us  [local(): stats_rim[0]]
    transpose x8 -> x3, local copies, waits for them, and re-layouts: 30.3 us -> 3.12 us  [pack_tiles(): shaped.transpose(axes_order)]
    select_n x4 -> x0, other arithmetic: 20.2 us -> none  [the longest x3 20.1 us: spread_tiles(): picked = jnp.take(field_map, row_index, axis=0)]
    dot_general x10 -> x0, matrix products: 18 us -> none  [the longest x1 3.12 us: local(): jnp.dot(attended_rows, w_out, preferred_element_type=jnp.float32)]
    transpose x2 -> x0, other arithmetic: 17.3 us -> none  [spread_tiles(): picked.transpose(axes_order)]
    convert_element_type x12 -> x1, local copies, waits for them, and re-layouts: 11.6 us -> 0.27 us  [local(): g_heads = mix('tf,hef->hte', grad_flat, out_heads).astype(jnp.bfloat16)]
    ppermute x6, waiting for transfers between devices: 3.54 us -> 13.6 us  [extended(): after = lax.ppermute(leading, axis, down)]
  transfers between devices with their start and end apart: 13 -> 13, of which waited for: 3 -> 5; matrix products, arithmetic and copies ran while one was open for 16% -> 11% of each run, Pallas kernels for 0% -> 0%
where the time goes in v3:
time: 439 us; the launch traced here: 432 us
  waiting for transfers between devices  243 us (55%)
  local copies, waits for them, and re-layouts  61.1 us (14%)
  matrix products  50.4 us (11%)
  starting transfers between devices  36.6 us (8%)
  other arithmetic  25 us (6%)
  between operations  15.5 us (4%)
    psum x1, waiting for transfers between devices, local(): summed = lax.psum(term_rows, ('tm', 'freq'))  227 us
    dot_general x19, matrix products, mix(): jnp.einsum(form, left_operand, right_operand, preferred_element_type=jnp....  50.4 us
    ppermute x6, starting transfers between devices, extended(): before = lax.ppermute(last, axis, up)  28.6 us
    unnamed x94, local copies, waits for them, and re-layouts  16.9 us
    ppermute x6, waiting for transfers between devices, extended(): after = lax.ppermute(leading, axis, down)  13.6 us
    slice x13, local copies, waits for them, and re-layouts, spread_tiles(): field_map[:, row_at:row_at + span_edge, col_at:col_at + span_edge]  9.79 us
  transfers between devices with their start and end apart: 13, of which 5 were waited for; matrix products, arithmetic and copies ran while one was open for 11% of the time, Pallas kernels for 0%

profile of v3, /device:TPU:0, one launch (start us, length us, event | category | flops | bytes accessed | tf_op | source)
XLA Modules:
  0.0 431.8 jit_solution(6596890589694733212)
XLA Ops:
  9.9 2.1 multiply_convert_fusion.5
  14.1 2.6 fusion.55
  24.5 5.7 %collective-permute-start = (bf16[2,8,6,16,128]{4,1,3,2,0:T(8,128)(2,1)}, bf16[2,8,6,16,128]{4,1,3,2,0:T(8,128)(2,1)}, u32[]{:S(2)}, u32[]{:S(2)}) collective-permute-start(bf16[2,8,6,16,128]{4,1,3,2,0:T(8,128)(2,1)} %get-tuple-element.31), channel_id=1, source_target_pairs={{0,8},{8,16},{16,24},{24,32},{32,40},{40,48},{48,56},{56,64},{64,7... | collective-permute-start | bytes 1179656 | tf_op jit(solution)/shard_map/ppermute | solution.py:25
  32.2 2.4 collective-permute-done.1
  34.6 2.6 pad_maximum_fusion.6
  37.2 4.3 collective-permute-start.2
  50.7 2.1 copy.145
  56.9 5.4 %collective-permute-start.6 = (bf16[2,8,28,6,128]{4,1,3,2,0:T(8,128)(2,1)S(1)}, bf16[2,8,28,6,128]{4,1,3,2,0:T(8,128)(2,1)S(1)}, u32[]{:S(2)}, u32[]{:S(2)}) collective-permute-start(bf16[2,8,28,6,128]{4,1,3,2,0:T(8,128)(2,1)S(1)} %copy.147), channel_id=1, source_target_pairs={{0,1},{1,2},{2,3},{3,4},{4,5},{5,6},{6,7},{8,9},{9,10},{10,11},{11... | collective-permute-start | bytes 2064392 | tf_op jit(solution)/shard_map/ppermute | solution.py:25
  62.3 6.8 %collective-permute-done.7 = bf16[2,8,28,6,128]{4,1,3,2,0:T(8,128)(2,1)} collective-permute-done((bf16[2,8,28,6,128]{4,1,3,2,0:T(8,128)(2,1)}, bf16[2,8,28,6,128]{4,1,3,2,0:T(8,128)(2,1)}, u32[]{:S(2)}, u32[]{:S(2)}) %collective-permute-start.7) | collective-permute-done | bytes 688160 | tf_op jit(solution)/shard_map/ppermute | solution.py:26
  73.2 3.1 pad_maximum_fusion.1
  76.3 2.6 slice_bitcast_fusion
  78.9 2.2 fusion.93
  88.2 2.3 copy_dynamic-update-slice_fusion.10
  90.5 2.2 copy_dynamic-update-slice_fusion.9
  93.7 3.6 fusion.48
  97.4 4.0 multiply_reduce_fusion
  102.0 6.2 %fusion.51 = bf16[8,4,64,128]{3,2,1,0:T(8,128)(2,1)S(1)} fusion(bf16[8,4,400,128]{3,2,1,0:T(8,128)(2,1)} %copy-done.12, f32[8,4,64,400]{3,2,1,0:T(8,128)} %get-tuple-element.54, f32[8,4,64]{2,1,0:T(4,128)} %copy-done.37, f32[8,4,64]{2,1,0:T(4,128)S(1)} %bitcast.285, f32[8,4,64,400]{3,2,1,0:T(8,128)} %copy-done.1, pred[4,64,400]{2,1,0:T(8,128)(4,1)S(1)} %broadcast_and_fusion), kind=kOutput, calls=%fused_computation.54 | convolution fusion | flops 216530944 | bytes 10473472 | tf_op jit(solution)/shard_map/hnqk,hnkd->hnqd/dot_general | solution.py:32
  109.4 9.4 %collective-permute-start.8 = (f32[2,8,6,16]{3,2,1,0:T(8,128)S(1)}, f32[2,8,6,16]{3,2,1,0:T(8,128)S(1)}, u32[]{:S(2)}, u32[]{:S(2)}) collective-permute-start(f32[2,8,6,16]{3,2,1,0:T(8,128)S(1)} %get-tuple-element.45), channel_id=1, source_target_pairs={{0,8},{8,16},{16,24},{24,32},{32,40},{40,48},{48,56},{56,64},{64,7... | collective-permute-start | bytes 18440 | tf_op jit(solution)/shard_map/ppermute | solution.py:25
  122.4 4.1 fusion.90
  129.4 2.7 fusion.102
  132.2 2.7 fusion.103
  135.9 3.7 fusion.101
  140.3 2.6 collective-permute-start.10
  144.7 2.1 collective-permute-done.10
  146.8 4.4 %collective-permute-done.11 = f32[2,8,28,6]{3,2,1,0:T(8,128)S(1)} collective-permute-done((f32[2,8,28,6]{3,2,1,0:T(8,128)S(1)}, f32[2,8,28,6]{3,2,1,0:T(8,128)S(1)}, u32[]{:S(2)}, u32[]{:S(2)}) %collective-permute-start.11) | collective-permute-done | bytes 10784 | tf_op jit(solution)/shard_map/ppermute | solution.py:26
  152.6 4.2 fusion.52
  157.7 7.2 %fusion.65 = bf16[8,4,64,128]{3,2,1,0:T(8,128)(2,1)} fusion(bf16[8,4,400,128]{3,2,1,0:T(8,128)(2,1)} %copy-done.11, f32[8,4,64,400]{3,2,1,0:T(8,128)} %fusion.101, bf16[8,4,64,128]{3,2,1,0:T(8,128)(2,1)S(1)} %bitcast.274, bf16[8,4,400,128]{3,2,1,0:T(8,128)(2,1)} %copy-done.30, f32[8,4,400]{2,1,0:T(4,128)S(1)} %copy.171, f32[8,4,400]{2,1,0:T(4,128)S(1)} %copy.161, ...), kind=kOutput, calls=%fused_computation.61 | convolution fusion | flops 425426944 | bytes 11006976 | tf_op jit(solution)/shard_map/hnkq,hnqd->hnkd/dot_general | solution.py:32
  174.4 7.2 %pad_maximum_fusion = f32[1024,4096]{0,1:T(8,128)} fusion(f32[1024,1024]{0,1:T(8,128)S(1)} %copy-done.3, f32[1024,1024]{0,1:T(8,128)S(1)} %fusion.105, f32[1024,1024]{0,1:T(8,128)S(1)} %fusion.104, f32[1024,1024]{0,1:T(8,128)S(1)} %copy-done.4), kind=kLoop, calls=%fused_computation | loop fusion | flops 12582912 | bytes 33554432 | tf_op jit(solution)/shard_map/concatenate | solution.py:201
  182.5 2.6 fusion.31
  190.7 227.5 %all-reduce.2.cloned.1.call-done = f32[1024,4096]{0,1:T(8,128)} async-done(((f32[1024,4096]{0,1:T(8,128)}), f32[1024,4096]{0,1:T(8,128)}) %all-reduce.2.cloned.1.call-update) | async-done | bytes 16777232 | tf_op jit(solution)/shard_map/psum | solution.py:210
  418.2 3.5 constant_dynamic-slice_fusion
  421.7 2.8 copy.181
  (202 shorter events, 69.3 us)
Async XLA Ops:
  7.2 4.8 %copy-start = (bf16[1024,1024]{1,0:T(8,128)(2,1)S(1)}, bf16[1024,1024]{1,0:T(8,128)(2,1)}, u32[]{:S(2)}) copy-start(bf16[1024,1024]{1,0:T(8,128)(2,1)} %param.10) | copy-start | bytes 6291460
  7.2 411.0 %all-reduce.2.cloned.1.call-start = ((), (), s32[]{:S(2)}) async-start(), calls=%async_computation | async-start | bytes 33554432 | tf_op jit(solution)/shard_map/psum | solution.py:210
  8.6 3.4 copy-start.31
  14.1 6.2 %copy-start.7 = (bf16[16,16,1024]{2,1,0:T(8,128)(2,1)S(1)}, bf16[16,16,1024]{2,1,0:T(8,128)(2,1)}, u32[]{:S(2)}) copy-start(bf16[16,16,1024]{2,1,0:T(8,128)(2,1)} %multiply_convert_fusion.5) | copy-start | bytes 1572868
  14.1 6.2 %copy-start.38 = (bf16[1024,1024]{1,0:T(8,128)(2,1)S(1)}, bf16[1024,1024]{1,0:T(8,128)(2,1)}, u32[]{:S(2)}) copy-start(bf16[1024,1024]{1,0:T(8,128)(2,1)} %param.9) | copy-start | bytes 6291460
  16.7 4.3 %copy-start.19 = (bf16[1024,1024]{1,0:T(8,128)(2,1)S(1)}, bf16[1024,1024]{1,0:T(8,128)(2,1)}, u32[]{:S(2)}) copy-start(bf16[1024,1024]{1,0:T(8,128)(2,1)} %param.8) | copy-start | bytes 6291460
  17.7 25.1 %collective-permute-start.4 = (bf16[2,8,6,16,128]{4,3,2,1,0:T(8,128)(2,1)}, bf16[2,8,6,16,128]{4,3,2,1,0:T(8,128)(2,1)S(1)}, u32[]{:S(2)}, u32[]{:S(2)}) collective-permute-start(bf16[2,8,6,16,128]{4,3,2,1,0:T(8,128)(2,1)} %get-tuple-element.29), channel_id=1, source_target_pairs={{0,8},{8,16},{16,24},{24,32},{32,40},{40,48},{48,56},{56,64},{64,7... | collective-permute-start | bytes 1179656 | tf_op jit(solution)/shard_map/ppermute | solution.py:25
  19.0 23.8 %collective-permute-start.5 = (bf16[2,8,6,16,128]{4,3,2,1,0:T(8,128)(2,1)}, bf16[2,8,6,16,128]{4,3,2,1,0:T(8,128)(2,1)}, u32[]{:S(2)}, u32[]{:S(2)}) collective-permute-start(bf16[2,8,6,16,128]{4,3,2,1,0:T(8,128)(2,1)} %get-tuple-element.30), channel_id=1, source_target_pairs={{8,0},{16,8},{24,16},{32,24},{40,32},{48,40},{56,48},{64,56},{72,6... | collective-permute-start | bytes 1179656 | tf_op jit(solution)/shard_map/ppermute | solution.py:26
  21.1 3.4 copy-start.23
  24.5 7.8 %collective-permute-start = (bf16[2,8,6,16,128]{4,1,3,2,0:T(8,128)(2,1)}, bf16[2,8,6,16,128]{4,1,3,2,0:T(8,128)(2,1)}, u32[]{:S(2)}, u32[]{:S(2)}) collective-permute-start(bf16[2,8,6,16,128]{4,1,3,2,0:T(8,128)(2,1)} %get-tuple-element.31), channel_id=1, source_target_pairs={{0,8},{8,16},{16,24},{24,32},{32,40},{40,48},{48,56},{56,64},{64,7... | collective-permute-start | bytes 1179656 | tf_op jit(solution)/shard_map/ppermute | solution.py:25
  30.2 4.4 %collective-permute-start.1 = (bf16[2,8,6,16,128]{4,1,3,2,0:T(8,128)(2,1)}, bf16[2,8,6,16,128]{4,1,3,2,0:T(8,128)(2,1)}, u32[]{:S(2)}, u32[]{:S(2)}) collective-permute-start(bf16[2,8,6,16,128]{4,1,3,2,0:T(8,128)(2,1)} %get-tuple-element.32), channel_id=1, source_target_pairs={{8,0},{16,8},{24,16},{32,24},{40,32},{48,40},{56,48},{64,56},{72,6... | collective-permute-start | bytes 1179656 | tf_op jit(solution)/shard_map/ppermute | solution.py:26
  37.2 33.1 %collective-permute-start.2 = (bf16[2,8,28,6,128]{4,1,3,2,0:T(8,128)(2,1)}, bf16[2,8,28,6,128]{4,1,3,2,0:T(8,128)(2,1)}, u32[]{:S(2)}, u32[]{:S(2)}) collective-permute-start(bf16[2,8,28,6,128]{4,1,3,2,0:T(8,128)(2,1)} %get-tuple-element.19), channel_id=1, source_target_pairs={{0,1},{1,2},{2,3},{3,4},{4,5},{5,6},{6,7},{8,9},{9,10},{10,11},{11... | collective-permute-start | bytes 2064392 | tf_op jit(solution)/shard_map/ppermute | solution.py:25
  41.5 28.9 %collective-permute-start.3 = (bf16[2,8,28,6,128]{4,1,3,2,0:T(8,128)(2,1)}, bf16[2,8,28,6,128]{4,1,3,2,0:T(8,128)(2,1)}, u32[]{:S(2)}, u32[]{:S(2)}) collective-permute-start(bf16[2,8,28,6,128]{4,1,3,2,0:T(8,128)(2,1)} %get-tuple-element.20), channel_id=1, source_target_pairs={{1,0},{2,1},{3,2},{4,3},{5,4},{6,5},{7,6},{9,8},{10,9},{11,10},{12... | collective-permute-start | bytes 2064392 | tf_op jit(solution)/shard_map/ppermute | solution.py:26
  46.7 22.3 %collective-permute-start.7 = (bf16[2,8,28,6,128]{4,1,3,2,0:T(8,128)(2,1)}, bf16[2,8,28,6,128]{4,1,3,2,0:T(8,128)(2,1)}, u32[]{:S(2)}, u32[]{:S(2)}) collective-permute-start(bf16[2,8,28,6,128]{4,1,3,2,0:T(8,128)(2,1)} %copy.148), channel_id=1, source_target_pairs={{1,0},{2,1},{3,2},{4,3},{5,4},{6,5},{7,6},{9,8},{10,9},{11,10},{12... | collective-permute-start | bytes 2064392 | tf_op jit(solution)/shard_map/ppermute | solution.py:26
  50.5 5.9 %copy-start.15 = (bf16[2,8,28,6,128]{4,3,2,1,0:T(8,128)(2,1)S(1)}, bf16[2,8,28,6,128]{4,3,2,1,0:T(8,128)(2,1)}, u32[]{:S(2)}) copy-start(bf16[2,8,28,6,128]{4,3,2,1,0:T(8,128)(2,1)} %get-tuple-element.17) | copy-start | bytes 2064388
  50.7 19.7 %copy-start.6 = (bf16[2,8,16,16,128]{4,1,3,2,0:T(8,128)(2,1)S(1)}, bf16[2,8,16,16,128]{4,1,3,2,0:T(8,128)(2,1)}, u32[]{:S(2)}) copy-start(bf16[2,8,16,16,128]{4,1,3,2,0:T(8,128)(2,1)} %copy-done.5) | copy-start | bytes 3145732
  56.9 15.6 %collective-permute-start.6 = (bf16[2,8,28,6,128]{4,1,3,2,0:T(8,128)(2,1)S(1)}, bf16[2,8,28,6,128]{4,1,3,2,0:T(8,128)(2,1)S(1)}, u32[]{:S(2)}, u32[]{:S(2)}) collective-permute-start(bf16[2,8,28,6,128]{4,1,3,2,0:T(8,128)(2,1)S(1)} %copy.147), channel_id=1, source_target_pairs={{0,1},{1,2},{2,3},{3,4},{4,5},{5,6},{6,7},{8,9},{9,10},{10,11},{11... | collective-permute-start | bytes 2064392 | tf_op jit(solution)/shard_map/ppermute | solution.py:25
  88.2 5.5 %copy-start.2 = (f32[8,4,64,400]{3,2,1,0:T(8,128)S(1)}, f32[8,4,64,400]{3,2,1,0:T(8,128)}, u32[]{:S(2)}) copy-start(f32[8,4,64,400]{3,2,1,0:T(8,128)} %copy-done.1) | copy-start | bytes 9830404
  93.7 3.7 copy-start.10
  93.7 3.7 copy-start.18
  97.4 24.0 %copy-start.21 = (bf16[8,2,2,8,8,128]{5,4,2,3,1,0:T(8,128)(2,1)}, bf16[8,2,2,8,8,128]{5,4,2,3,1,0:T(8,128)(2,1)S(1)}, u32[]{:S(2)}) copy-start(bf16[8,2,2,8,8,128]{5,4,2,3,1,0:T(8,128)(2,1)S(1)} %copy.140) | copy-start | bytes 1572868
  109.4 30.7 %collective-permute-start.8 = (f32[2,8,6,16]{3,2,1,0:T(8,128)S(1)}, f32[2,8,6,16]{3,2,1,0:T(8,128)S(1)}, u32[]{:S(2)}, u32[]{:S(2)}) collective-permute-start(f32[2,8,6,16]{3,2,1,0:T(8,128)S(1)} %get-tuple-element.45), channel_id=1, source_target_pairs={{0,8},{8,16},{16,24},{24,32},{32,40},{40,48},{48,56},{56,64},{64,7... | collective-permute-start | bytes 18440 | tf_op jit(solution)/shard_map/ppermute | solution.py:25
  118.8 21.3 %collective-permute-start.9 = (f32[2,8,6,16]{3,2,1,0:T(8,128)S(1)}, f32[2,8,6,16]{3,2,1,0:T(8,128)S(1)}, u32[]{:S(2)}, u32[]{:S(2)}) collective-permute-start(f32[2,8,6,16]{3,2,1,0:T(8,128)S(1)} %get-tuple-element.46), channel_id=1, source_target_pairs={{8,0},{16,8},{24,16},{32,24},{40,32},{48,40},{56,48},{64,56},{72,6... | collective-permute-start | bytes 18440 | tf_op jit(solution)/shard_map/ppermute | solution.py:26
  135.4 4.1 copy-start.11
  140.3 6.4 %collective-permute-start.10 = (f32[2,8,28,6]{3,2,1,0:T(8,128)S(1)}, f32[2,8,28,6]{3,2,1,0:T(8,128)S(1)}, u32[]{:S(2)}, u32[]{:S(2)}) collective-permute-start(f32[2,8,28,6]{3,2,1,0:T(8,128)S(1)} %get-tuple-element.35), channel_id=1, source_target_pairs={{0,1},{1,2},{2,3},{3,4},{4,5},{5,6},{6,7},{8,9},{9,10},{10,11},{11... | collective-permute-start | bytes 32264 | tf_op jit(solution)/shard_map/ppermute | solution.py:25
  142.9 8.3 %collective-permute-start.11 = (f32[2,8,28,6]{3,2,1,0:T(8,128)S(1)}, f32[2,8,28,6]{3,2,1,0:T(8,128)S(1)}, u32[]{:S(2)}, u32[]{:S(2)}) collective-permute-start(f32[2,8,28,6]{3,2,1,0:T(8,128)S(1)} %get-tuple-element.36), channel_id=1, source_target_pairs={{1,0},{2,1},{3,2},{4,3},{5,4},{6,5},{7,6},{9,8},{10,9},{11,10},{12... | collective-permute-start | bytes 32264 | tf_op jit(solution)/shard_map/ppermute | solution.py:26
  144.6 6.9 %copy-start.30 = (bf16[8,4,400,128]{3,2,1,0:T(8,128)(2,1)}, bf16[8,4,400,128]{3,2,1,0:T(8,128)(2,1)S(1)}, u32[]{:S(2)}) copy-start(bf16[8,4,400,128]{3,2,1,0:T(8,128)(2,1)S(1)} %copy_dynamic-update-slice_fusion) | copy-start | bytes 9830404
  152.5 5.2 %copy-start.29 = (bf16[8,2,8,2,8,128]{5,4,2,3,1,0:T(8,128)(2,1)S(1)}, bf16[8,2,8,2,8,128]{5,4,2,3,1,0:T(8,128)(2,1)}, u32[]{:S(2)}) copy-start(bf16[8,2,8,2,8,128]{5,4,2,3,1,0:T(8,128)(2,1)} %copy.162) | copy-start | bytes 1572868
  152.5 5.2 %copy-start.34 = (pred[64,400]{1,0:T(8,128)(4,1)S(1)}, pred[64,400]{1,0:T(8,128)(4,1)}, u32[]{:S(2)}) copy-start(pred[64,400]{1,0:T(8,128)(4,1)} %copy-done.33) | copy-start | bytes 76804
  171.0 3.5 copy-start.4
  182.4 2.8 copy-start.9
  182.5 4.2 copy-start.20
  (21 other events, 33.3 us)
Sparse Core Ops, SparseCore 0:
  181.8 236.3 all-reduce.1
